TPU v7x, 32 devices: a whole 2x2x4 slice. The times are simulated.
32 devices in a mesh: rows: 4 (over x, core), aux: 8 (over z, y).
Axes of the slice: x: 2, y: 2, z: 4, core: 2. Of those that a mesh axis runs over, the one named last changes fastest.
Arguments:
- b_rows: bfloat16 [6144, 8192], P(('rows', 'aux')), may hold values from -0.079589844 to 0.079589844
- pair_index: int32 [6144], P(('rows', 'aux')), may hold values from 0 to 6143, each once
- e_occ: float32 [512], replicated, may hold values from -3 to -0.5
- e_vir: float32 [1536], replicated, may hold values from 0.2 to 3
- occ_batch: int32 [1], replicated, may hold values from 0 to 127
- freq: float32 [1], replicated, may hold values from 0.3 to 3
Outputs:
- q_matrix: float32 [8192, 8192], P('aux', 'rows')
All inputs are finite; a program needn't handle non-finite values.
Results may differ from a plain program's by a relative error of at most 0.0022.
Values may be sent and summed in bfloat16 or wider, within the bound.
No kernel may reach another device: no remote copies, remote signals or barrier semaphores. Data moves between devices by JAX's collectives and lax.ppermute only.
A program may use at most 192 MiB of HBM per device.

v0:
```python
import jax
import jax.numpy as jnp
from jax import lax
from jax.sharding import PartitionSpec as P

NVIR = 1536
NOCC_B = 4


def row_weights(pairs, e_occ, e_vir, occ_batch, freq):
    batch_start = occ_batch[0] * NOCC_B
    e_batch = lax.dynamic_slice_in_dim(e_occ, batch_start, NOCC_B, 0)
    occ = pairs // NVIR
    vir = pairs % NVIR
    occ_hit = occ[:, None] == jnp.arange(NOCC_B, dtype=jnp.int32)[None, :]
    vir_hit = vir[:, None] == jnp.arange(e_vir.shape[0], dtype=jnp.int32)[None, :]
    e_low = jnp.sum(jnp.where(occ_hit, e_batch[None, :], 0.0), axis=1)
    e_high = jnp.sum(jnp.where(vir_hit, e_vir[None, :], 0.0), axis=1)
    delta = e_high - e_low
    return 2.0 * delta / (delta * delta + freq[0] * freq[0])


def contract(left, right):
    return lax.dot_general(
        left, right, (((0,), (0,)), ((), ())), preferred_element_type=jnp.float32
    )


def body(b_rows, pair_index, e_occ, e_vir, occ_batch, freq):
    group_pairs = lax.all_gather(pair_index, "aux", axis=0, tiled=True)
    regrouped = lax.all_to_all(b_rows, "aux", split_axis=1, concat_axis=0, tiled=True)
    weight = row_weights(group_pairs, e_occ, e_vir, occ_batch, freq)
    scaled = (weight[:, None] * regrouped.astype(jnp.float32)).astype(jnp.bfloat16)
    partial_value = contract(scaled, lax.all_gather(regrouped, "aux", axis=1, tiled=True))
    return lax.psum_scatter(partial_value, "rows", scatter_dimension=1, tiled=True)


def solution(mesh):
    placed = (P(("rows", "aux"), None), P(("rows", "aux")), P(), P(), P(), P())
    return jax.shard_map(
        body, mesh=mesh, in_specs=placed, out_specs=P("aux", "rows"), check_vma=False
    )
```

profile of v0, /device:TPU:0, one launch (start us, length us, event | category | flops | bytes accessed | tf_op | source)
XLA Modules:
  0.0 842.8 jit_solution(14496598981891353015)
XLA Ops:
  6.5 0.0 copy-start.2
  6.5 0.0 copy-start
  6.5 0.0 copy-start.1
  6.5 0.0 all-gather.2.cloned.1.call-start
  6.5 2.4 copy.12
  8.9 77.9 %all_to_all.19 = bf16[192,8,1024]{2,0,1:T(8,128)(2,1)} all-to-all(bf16[192,8,1024]{2,0,1:T(8,128)(2,1)S(1)} %bitcast.13), channel_id=1, replica_groups=mesh['rows'=4,'aux'=8] {'aux'}, dimensions={1} | all-to-all | bytes 6291456 | tf_op jit(solution)/shard_map/all_to_all | solution.py:31
  86.8 0.0 all-gather.2.cloned.1.call-update
  86.8 0.0 reduce-scatter.2.cloned.1.call-start
  88.2 0.0 copy-done.2
  88.2 0.6 dynamic-slice
  89.4 0.8 dynamic_slice.3
  90.2 0.0 copy-done
  90.2 0.2 dynamic-update-slice
  90.4 42.0 %all-reduce = s32[1536]{0:T(1024)S(1)} all-reduce(s32[1536]{0:T(1024)S(1)} %dynamic-update-slice), channel_id=1, replica_groups=mesh['rows'=4,'aux'=8] {'aux'}, use_global_device_ids=true, to_apply=%add | all-reduce | flops 1536 | bytes 12288
  132.4 0.1 select_reduce_fusion.1
  132.5 0.0 copy-done.1
  132.5 1.3 select_reduce_fusion
  133.8 432.7 %all-gather.2.cloned.1.call-done = bf16[1536,8192]{1,0:T(8,128)(2,1)} async-done(((bf16[1536,1024]{1,0:T(8,128)(2,1)}), bf16[1536,8192]{1,0:T(8,128)(2,1)}) %all-gather.2.cloned.1.call-update) | async-done | bytes 25165840 | tf_op jit(solution)/shard_map/all_gather | solution.py:34
  566.5 34.5 %fusion = f32[1024,8192]{1,0:T(8,128)} fusion(bf16[1536,8192]{1,0:T(8,128)(2,1)} %all-gather.2.cloned.1.call-done, bf16[1536,1024]{1,0:T(8,128)(2,1)} %bitcast.12, f32[1536]{0:T(1024)S(1)} %add_divide_fusion), kind=kOutput, calls=%fused_computation.3 | convolution fusion | flops 25774522368 | bytes 61872128 | tf_op jit(solution)/shard_map/dot_general | solution.py:24
  601.0 0.0 reduce-scatter.2.cloned.1.call-update
  601.0 234.9 %reduce-scatter.2.cloned.1.call-done = f32[1024,2048]{1,0:T(8,128)} async-done(((f32[1024,8192]{1,0:T(8,128)}), f32[1024,2048]{1,0:T(8,128)}) %reduce-scatter.2.cloned.1.call-update) | async-done | bytes 8388624 | tf_op jit(solution)/shard_map/reduce_scatter | solution.py:35
  (3 shorter events, 0.0 us)
Async XLA Ops:
  6.5 81.6 %copy-start.2 = (u32[32]{0:T(128)S(1)}, u32[32]{0:T(128)}, u32[]{:S(2)}) copy-start(u32[32]{0:T(128)} %constant.32) | copy-start | bytes 388
  6.5 83.7 %copy-start = (s32[192]{0:T(256)S(1)}, s32[192]{0:T(256)}, u32[]{:S(2)}) copy-start(s32[192]{0:T(256)} %param.7) | copy-start | bytes 2308
  6.5 126.0 %copy-start.1 = (f32[1536]{0:T(1024)S(1)}, f32[1536]{0:T(1024)}, u32[]{:S(2)}) copy-start(f32[1536]{0:T(1024)} %param.9) | copy-start | bytes 18436
  6.5 560.0 %all-gather.2.cloned.1.call-start = ((), (), s32[]{:S(2)}) async-start(), calls=%async_computation.2 | async-start | bytes 28311552 | tf_op jit(solution)/shard_map/all_gather | solution.py:34
  86.8 749.1 %reduce-scatter.2.cloned.1.call-start = ((), (), s32[]{:S(2)}) async-start(), calls=%async_computation.3 | async-start | bytes 41943040 | tf_op jit(solution)/shard_map/reduce_scatter | solution.py:35
Sparse Core Ops, SparseCore 0:
  86.9 479.5 all-gather.1
  601.2 234.7 reduce-scatter.1
where the time goes:
time: 843 us
  waiting for transfers between devices  668 us (79%)
  blocking collectives  120 us (14%)
  matrix products  34.5 us (4%)
  between operations  15.4 us (2%)
    all_gather x1, waiting for transfers between devices, body(): lax.all_gather(regrouped, 'aux', axis=1, tiled=True)  433 us
    reduce_scatter x1, waiting for transfers between devices, body(): lax.psum_scatter(partial_value, 'rows', scatter_dimension=1, tiled=True)  235 us
    all_to_all x1, blocking collectives, body(): lax.all_to_all(b_rows, 'aux', split_axis=1, concat_axis=0, tiled=True)  77.9 us
    unnamed x1, blocking collectives  42 us
    dot_general x1, matrix products, contract(): lax.dot_general(left, right, (((0,), (0,)), ((), ())), preferred_element_...  34.5 us
  transfers between devices with their start and end apart: 2, of which 2 were waited for; matrix products, arithmetic and copies ran while one was open for 0% of the time, Pallas kernels for 0%

commit v1 on v0

v1 whole, which is shorter than its diff:
```python
import jax
import jax.numpy as jnp
from jax import lax
from jax.sharding import Mesh, PartitionSpec as P

NVIR = 1536
NOCC_B = 4


def row_weights(pairs, e_occ, e_vir, occ_batch, freq):
    batch_start = occ_batch[0] * NOCC_B
    e_batch = lax.dynamic_slice_in_dim(e_occ, batch_start, NOCC_B, 0)
    occ = pairs // NVIR
    vir = pairs % NVIR
    occ_hit = occ[:, None] == jnp.arange(NOCC_B, dtype=jnp.int32)[None, :]
    vir_hit = vir[:, None] == jnp.arange(e_vir.shape[0], dtype=jnp.int32)[None, :]
    e_low = jnp.sum(jnp.where(occ_hit, e_batch[None, :], 0.0), axis=1)
    e_high = jnp.sum(jnp.where(vir_hit, e_vir[None, :], 0.0), axis=1)
    delta = e_high - e_low
    return 2.0 * delta / (delta * delta + freq[0] * freq[0])


def contract(left, right):
    return lax.dot_general(
        left, right, (((0,), (0,)), ((), ())), preferred_element_type=jnp.float32
    )


def make_body(n_rx, n_rc, n_az, n_ay):
    def body(b_rows, pair_index, e_occ, e_vir, occ_batch, freq):
        naux = b_rows.shape[1]
        width = naux // (n_az * n_ay)
        rw = naux // (n_rx * n_rc)
        weight = row_weights(pair_index, e_occ, e_vir, occ_batch, freq)
        weight = lax.all_gather(weight, "az", axis=0, tiled=True)
        weight = lax.all_gather(weight, "ay", axis=0, tiled=True)
        group = lax.all_gather(b_rows, "az", axis=0, tiled=True)
        group = lax.all_gather(group, "ay", axis=0, tiled=True)
        a = lax.axis_index("az") * n_ay + lax.axis_index("ay")
        own = lax.dynamic_slice_in_dim(group, a * width, width, axis=1)
        scaled = (weight[:, None] * own.astype(jnp.float32)).astype(jnp.bfloat16)
        blocks = group.reshape(group.shape[0], n_rx, n_rc, rw)
        partial_value = jnp.einsum(
            "kp,kxcr->cxpr", scaled, blocks, preferred_element_type=jnp.float32
        )
        partial_value = lax.psum_scatter(partial_value, "rc", scatter_dimension=0, tiled=True)
        partial_value = lax.psum_scatter(partial_value, "rx", scatter_dimension=1, tiled=True)
        return partial_value.reshape(width, rw)

    return body


def solution(mesh):
    n_rows = mesh.shape["rows"]
    n_aux = mesh.shape["aux"]
    n_rc = 2 if n_rows % 2 == 0 else 1
    n_ay = 2 if n_aux % 2 == 0 else 1
    n_rx = n_rows // n_rc
    n_az = n_aux // n_ay
    split = Mesh(mesh.devices.reshape(n_rx, n_rc, n_az, n_ay), ("rx", "rc", "az", "ay"))
    rows_all = ("rx", "rc", "az", "ay")
    placed = (P(rows_all, None), P(rows_all), P(), P(), P(), P())
    return jax.shard_map(
        make_body(n_rx, n_rc, n_az, n_ay),
        mesh=split,
        in_specs=placed,
        out_specs=P(("az", "ay"), ("rx", "rc")),
        check_vma=False,
    )
```

time: 843 us -> 887 us (1.052)
  waiting for transfers between devices: 668 us -> 793 us
  blocking collectives: 120 us -> 13 us
  local copies, waits for them, and re-layouts: 3.93 us -> 31.4 us
    unnamed x2 -> x5, waiting for transfers between devices: 0.03 us -> 102 us
    all_to_all x1 -> x0, blocking collectives: 77.9 us -> none  [body(): lax.all_to_all(b_rows, 'aux', split_axis=1, concat_axis=0, tiled=True)]
    all_gather x1 -> x2, waiting for transfers between devices: 433 us -> 500 us  [the longest x1 278 us: body(): group = lax.all_gather(group, 'ay', axis=0, tiled=True)]
    reduce_scatter x1, waiting for transfers between devices: 235 us -> 191 us  [body(): lax.psum_scatter(partial_value, 'rx', scatter_dimension=1, tiled=True)]
    unnamed x1, blocking collectives: 42 us -> 8.63 us
    all_gather x0 -> x1, local copies, waits for them, and re-layouts: none -> 16.6 us  [body(): group = lax.all_gather(b_rows, 'az', axis=0, tiled=True)]
    unnamed x9 -> x14, local copies, waits for them, and re-layouts: 0.82 us -> 14 us
  transfers between devices with their start and end apart: 2 -> 4, of which waited for: 2 -> 4; matrix products, arithmetic and copies ran while one was open for 0% -> 0% of each run, Pallas kernels for 0% -> 0%
where the time goes in v1:
time: 887 us; the launch traced here: 886 us
  waiting for transfers between devices  793 us (89%)
  matrix products  33.8 us (4%)
  local copies, waits for them, and re-layouts  31.4 us (4%)
  between operations  15.1 us (2%)
  blocking collectives  13 us (1%)
    all_gather x1, waiting for transfers between devices, body(): group = lax.all_gather(group, 'ay', axis=0, tiled=True)  278 us
    all_gather x1, waiting for transfers between devices, body(): group = lax.all_gather(b_rows, 'az', axis=0, tiled=True)  223 us
    reduce_scatter x1, waiting for transfers between devices, body(): lax.psum_scatter(partial_value, 'rx', scatter_dimension=1, tiled=True)  191 us
    unnamed x5, waiting for transfers between devices  102 us
    dot_general x1, matrix products, body(): jnp.einsum('kp,kxcr->cxpr', scaled, blocks, preferred_element_type=jnp.fl...  33.8 us
  transfers between devices with their start and end apart: 4, of which 4 were waited for; matrix products, arithmetic and copies ran while one was open for 0% of the time, Pallas kernels for 0%

profile of v1, /device:TPU:0, one launch (start us, length us, event | category | flops | bytes accessed | tf_op | source)
XLA Modules:
  0.0 886.5 jit_solution(946498511156553110)
XLA Ops:
  6.5 0.0 all-gather.4.cloned.1.call-start
  6.5 0.7 all-gather.4.cloned.1.call-update
  7.3 0.0 all-gather.6.cloned.1.call-start
  7.3 222.6 %all-gather.4.cloned.1.call-done = bf16[768,8192]{1,0:T(8,128)(2,1)} async-done(((bf16[192,8192]{1,0:T(8,128)(2,1)}), bf16[768,8192]{1,0:T(8,128)(2,1)}) %all-gather.4.cloned.1.call-update) | async-done | bytes 12582928 | tf_op jit(solution)/shard_map/all_gather | solution.py:37
  229.9 16.6 %copy.12 = bf16[768,8192]{0,1:T(8,128)(2,1)} copy(bf16[768,8192]{1,0:T(8,128)(2,1)} %all-gather.4.cloned.1.call-done) | data formatting | bytes 25165824 | tf_op jit(solution)/shard_map/all_gather | solution.py:37
  246.5 0.0 copy-start.3
  246.5 0.0 copy-start.1
  246.5 0.0 copy-start
  246.5 0.0 all-gather.6.cloned.1.call-update
  246.5 0.0 all-reduce.4.cloned.1.call-start
  247.9 0.8 dynamic_slice.6
  248.6 0.0 copy-done.3
  248.6 0.6 dynamic-slice
  249.9 0.0 copy-done.1
  249.9 0.1 select_reduce_fusion.1
  250.0 0.0 copy-done
  250.0 0.3 select_reduce_fusion
  250.3 0.1 divide_dynamic-update-slice_fusion
  250.4 8.6 all-reduce
  259.0 4.3 all-gather
  263.4 277.7 %all-gather.6.cloned.1.call-done = bf16[1536,8192]{0,1:T(8,128)(2,1)} async-done(((bf16[768,8192]{0,1:T(8,128)(2,1)}), bf16[1536,8192]{0,1:T(8,128)(2,1)}) %all-gather.6.cloned.1.call-update) | async-done | bytes 25165840 | tf_op jit(solution)/shard_map/all_gather | solution.py:38
  541.1 33.8 %convolution_bitcast_fusion = f32[2,2,1024,2048]{3,2,0,1:T(8,128)} fusion(bf16[1536,2,2,2048]{0,3,2,1:T(8,128)(2,1)} %bitcast.20, bf16[1536,8192]{0,1:T(8,128)(2,1)} %all-gather.6.cloned.1.call-done, s32[]{:T(128)S(6)} %select_n.31, f32[1536]{0:T(1024)S(1)} %reshape.20), kind=kOutput, calls=%fused_computation | convolution fusion | flops 25774522368 | bytes 61872132 | tf_op jit(solution)/shard_map/kp,kxcr->cxpr/dot_general | solution.py:43
  574.9 0.0 copy-start.2
  574.9 0.0 all-reduce.4.cloned.1.call-update
  574.9 0.0 reduce-scatter.5.cloned.1.call-start
  575.0 0.6 copy-done.2
  575.5 0.6 dynamic-slice.1
  576.1 101.0 %all-reduce.4.cloned.1.call-done = f32[2,2,1024,2048]{3,2,0,1:T(8,128)} async-done(((f32[2,2,1024,2048]{3,2,0,1:T(8,128)}), f32[2,2,1024,2048]{3,2,0,1:T(8,128)}) %all-reduce.4.cloned.1.call-update) | async-done | bytes 33554448
  677.1 12.3 %constant_dynamic-slice_fusion = f32[1,2,1024,2048]{3,2,0,1:T(8,128)} fusion(f32[2,2,1024,2048]{3,2,0,1:T(8,128)} %all-reduce.4.cloned.1.call-done, u32[]{:T(128)} %bitcast.15), kind=kLoop, calls=%fused_computation.13 | loop fusion | bytes 33554436
  689.3 0.0 reduce-scatter.5.cloned.1.call-update
  689.4 190.6 %reduce-scatter.5.cloned.1.call-done = f32[1,1,1024,2048]{3,2,0,1:T(8,128)} async-done(((f32[1,2,1024,2048]{3,2,0,1:T(8,128)}), f32[1,1,1024,2048]{3,2,0,1:T(8,128)}) %reduce-scatter.5.cloned.1.call-update) | async-done | bytes 8388624 | tf_op jit(solution)/shard_map/reduce_scatter | solution.py:47
  (5 shorter events, 0.1 us)
Async XLA Ops:
  6.5 223.3 %all-gather.4.cloned.1.call-start = ((), (), s32[]{:S(2)}) async-start(), calls=%async_computation.1 | async-start | bytes 15728640 | tf_op jit(solution)/shard_map/all_gather | solution.py:37
  7.3 533.8 %all-gather.6.cloned.1.call-start = ((), (), s32[]{:S(2)}) async-start(), calls=%async_computation.2 | async-start | bytes 37748736 | tf_op jit(solution)/shard_map/all_gather | solution.py:38
  246.5 2.1 copy-start.3
  246.5 3.4 copy-start.1
  246.5 3.5 copy-start
  246.5 430.6 %all-reduce.4.cloned.1.call-start = ((), (), s32[]{:S(2)}) async-start(), calls=%async_computation.4 | async-start | bytes 67108864
  574.9 0.7 copy-start.2
  574.9 305.0 %reduce-scatter.5.cloned.1.call-start = ((), (), s32[]{:S(2)}) async-start(), calls=%async_computation.3 | async-start | bytes 25165824 | tf_op jit(solution)/shard_map/reduce_scatter | solution.py:47
Sparse Core Ops, SparseCore 0:
  8.9 220.8 all-gather.3
  246.6 294.3 all-gather.5
  575.0 102.0 all-reduce.3
  689.5 190.3 reduce-scatter.4

commit v2 on v1

--- a/solution.py
+++ b/solution.py
@@ -5,6 +5,7 @@
 
 NVIR = 1536
 NOCC_B = 4
+CHUNKS = 4
 
 
 def row_weights(pairs, e_occ, e_vir, occ_batch, freq):
@@ -26,25 +27,49 @@
     )
 
 
+def swap(x, axis):
+    return lax.ppermute(x, axis, [(0, 1), (1, 0)])
+
+
+def reduce_pair(parts, axis, n, dim, send_dtype):
+    if n != 2:
+        return lax.psum_scatter(parts, axis, scatter_dimension=dim, tiled=True)
+    me = lax.axis_index(axis)
+    keep = lax.dynamic_slice_in_dim(parts, me, 1, axis=dim)
+    give = lax.dynamic_slice_in_dim(parts, 1 - me, 1, axis=dim)
+    got = swap(give.astype(send_dtype), axis)
+    return keep + got.astype(keep.dtype)
+
+
 def make_body(n_rx, n_rc, n_az, n_ay):
     def body(b_rows, pair_index, e_occ, e_vir, occ_batch, freq):
         naux = b_rows.shape[1]
         width = naux // (n_az * n_ay)
         rw = naux // (n_rx * n_rc)
+        chunks = CHUNKS if naux % (CHUNKS * 128) == 0 else 1
+        cw = naux // chunks
         weight = row_weights(pair_index, e_occ, e_vir, occ_batch, freq)
         weight = lax.all_gather(weight, "az", axis=0, tiled=True)
-        weight = lax.all_gather(weight, "ay", axis=0, tiled=True)
-        group = lax.all_gather(b_rows, "az", axis=0, tiled=True)
-        group = lax.all_gather(group, "ay", axis=0, tiled=True)
+        mine, theirs = [], []
+        for j in range(chunks):
+            piece = lax.all_gather(b_rows[:, j * cw:(j + 1) * cw], "az", axis=0, tiled=True)
+            mine.append(piece)
+            theirs.append(swap(piece, "ay") if n_ay == 2 else piece)
+        if n_ay == 2:
+            weight = jnp.concatenate([weight, swap(weight, "ay")], axis=0)
+            order = lax.axis_index("ay")
+            mine_all = jnp.concatenate(mine, axis=1)
+            theirs_all = jnp.concatenate(theirs, axis=1)
+            group = jnp.concatenate([mine_all, theirs_all], axis=0)
+        else:
+            group = lax.all_gather(jnp.concatenate(mine, axis=1), "ay", axis=0, tiled=True)
+            weight = lax.all_gather(weight, "ay", axis=0, tiled=True)
         a = lax.axis_index("az") * n_ay + lax.axis_index("ay")
         own = lax.dynamic_slice_in_dim(group, a * width, width, axis=1)
         scaled = (weight[:, None] * own.astype(jnp.float32)).astype(jnp.bfloat16)
-        blocks = group.reshape(group.shape[0], n_rx, n_rc, rw)
-        partial_value = jnp.einsum(
-            "kp,kxcr->cxpr", scaled, blocks, preferred_element_type=jnp.float32
-        )
-        partial_value = lax.psum_scatter(partial_value, "rc", scatter_dimension=0, tiled=True)
-        partial_value = lax.psum_scatter(partial_value, "rx", scatter_dimension=1, tiled=True)
+        partial_value = contract(scaled, group).reshape(width, n_rx, n_rc, rw)
+        partial_value = reduce_pair(partial_value, "rc", n_rc, 2, jnp.float32)
+        partial_value = reduce_pair(partial_value, "rx", n_rx, 1, jnp.bfloat16)
         return partial_value.reshape(width, rw)
 
     return body

time: 887 us -> 694 us (0.78)
  waiting for transfers between devices: 793 us -> 434 us
  local copies, waits for them, and re-layouts: 31.4 us -> 114 us
  other arithmetic: 0.51 us -> 77.8 us
    all_gather x2 -> x4, waiting for transfers between devices: 500 us -> 251 us  [body(): lax.all_gather(b_rows[:, j * cw:(j + 1) * cw], 'az', axis=0, tiled=True)]
    reduce_scatter x1 -> x0, waiting for transfers between devices: 191 us -> none  [body(): lax.psum_scatter(partial_value, 'rx', scatter_dimension=1, tiled=True)]
    ppermute x0 -> x7, waiting for transfers between devices: none -> 181 us  [swap(): return lax.ppermute(x, axis, [(0, 1), (1, 0)])]
    unnamed x5 -> x4, waiting for transfers between devices: 102 us -> 1.91 us
    concatenate x0 -> x2, other arithmetic: none -> 51.3 us  [the longest x1 51.3 us: body(): group = jnp.concatenate([mine_all, theirs_all], axis=0)]
    reshape x0 -> x1, local copies, waits for them, and re-layouts: none -> 42.6 us  [body(): partial_value = contract(scaled, group).reshape(width, n_rx, n_rc, rw)]
    dynamic_slice x0 -> x1, local copies, waits for them, and re-layouts: none -> 41.3 us  [reduce_pair(): keep = lax.dynamic_slice_in_dim(parts, me, 1, axis=dim)]
    all_gather x1 -> x0, local copies, waits for them, and re-layouts: 16.6 us -> none  [body(): group = lax.all_gather(b_rows, 'az', axis=0, tiled=True)]
  transfers between devices with their start and end apart: 4 -> 11, of which waited for: 4 -> 7; matrix products, arithmetic and copies ran while one was open for 0% -> 1% of each run, Pallas kernels for 0% -> 0%
where the time goes in v2:
time: 694 us; the launch traced here: 693 us
  waiting for transfers between devices  434 us (63%)
  local copies, waits for them, and re-layouts  114 us (16%)
  other arithmetic  77.8 us (11%)
  matrix products  34.6 us (5%)
  between operations  15.1 us (2%)
  blocking collectives  9.29 us (1%)
  starting transfers between devices  7.85 us (1%)
    all_gather x4, waiting for transfers between devices, body(): lax.all_gather(b_rows[:, j * cw:(j + 1) * cw], 'az', axis=0, tiled=True)  251 us
    ppermute x7, waiting for transfers between devices, swap(): return lax.ppermute(x, axis, [(0, 1), (1, 0)])  181 us
    concatenate x1, other arithmetic, body(): group = jnp.concatenate([mine_all, theirs_all], axis=0)  51.3 us
    reshape x1, local copies, waits for them, and re-layouts, body(): partial_value = contract(scaled, group).reshape(width, n_rx, n_rc, rw)  42.6 us
    dynamic_slice x1, local copies, waits for them, and re-layouts, reduce_pair(): keep = lax.dynamic_slice_in_dim(parts, me, 1, axis=dim)  41.3 us
    dot_general x1, matrix products, contract(): lax.dot_general(left, right, (((0,), (0,)), ((), ())), preferred_element_...  34.6 us
    unnamed x5, local copies, waits for them, and re-layouts  22.7 us
    add x1, other arithmetic, reduce_pair(): return keep + got.astype(keep.dtype)  14.5 us
  transfers between devices with their start and end apart: 11, of which 7 were waited for; matrix products, arithmetic and copies ran while one was open for 1% of the time, Pallas kernels for 0%

profile of v2, /device:TPU:0, one launch (start us, length us, event | category | flops | bytes accessed | tf_op | source)
XLA Modules:
  0.0 692.5 jit_solution(9391411062405025296)
XLA Ops:
  6.5 0.0 all-gather.5.cloned.1.call-start
  6.5 3.7 fusion.4
  10.2 0.0 all-gather.5.cloned.1.call-update
  10.2 0.0 all-gather.7.cloned.1.call-start
  10.3 0.7 all-gather.7.cloned.1.call-update
  11.0 0.0 all-gather.9.cloned.1.call-start
  11.0 0.7 all-gather.9.cloned.1.call-update
  11.7 0.0 all-gather.11.cloned.1.call-start
  11.8 0.5 all-gather.11.cloned.1.call-update
  12.3 64.3 %all-gather.5.cloned.1.call-done = bf16[768,2048]{1,0:T(8,128)(2,1)} async-done(((bf16[192,2048]{1,0:T(8,128)(2,1)}), bf16[768,2048]{1,0:T(8,128)(2,1)}) %all-gather.5.cloned.1.call-update) | async-done | bytes 3145744 | tf_op jit(solution)/shard_map/all_gather | solution.py:55
  76.6 1.5 collective-permute-start.1
  78.1 62.3 %all-gather.7.cloned.1.call-done = bf16[768,2048]{1,0:T(8,128)(2,1)} async-done(((bf16[192,2048]{1,0:T(8,128)(2,1)}), bf16[768,2048]{1,0:T(8,128)(2,1)}) %all-gather.7.cloned.1.call-update) | async-done | bytes 3145744 | tf_op jit(solution)/shard_map/all_gather | solution.py:55
  140.3 1.5 collective-permute-start.2
  141.8 62.3 %all-gather.9.cloned.1.call-done = bf16[768,2048]{1,0:T(8,128)(2,1)} async-done(((bf16[192,2048]{1,0:T(8,128)(2,1)}), bf16[768,2048]{1,0:T(8,128)(2,1)}) %all-gather.9.cloned.1.call-update) | async-done | bytes 3145744 | tf_op jit(solution)/shard_map/all_gather | solution.py:55
  204.1 1.5 collective-permute-start.3
  205.6 62.1 %all-gather.11.cloned.1.call-done = bf16[768,2048]{1,0:T(8,128)(2,1)} async-done(((bf16[192,2048]{1,0:T(8,128)(2,1)}), bf16[768,2048]{1,0:T(8,128)(2,1)}) %all-gather.11.cloned.1.call-update) | async-done | bytes 3145744 | tf_op jit(solution)/shard_map/all_gather | solution.py:55
  267.7 1.5 collective-permute-start.4
  270.5 0.8 dynamic_slice.18
  271.2 1.2 dynamic-slice
  273.1 0.7 and_select_fusion
  273.8 0.1 select_reduce_fusion.1
  273.9 1.0 select_reduce_fusion
  274.9 0.1 divide_dynamic-update-slice_fusion
  275.0 9.3 %all-reduce = f32[768]{0:T(1024)S(1)} all-reduce(f32[768]{0:T(1024)S(1)} %divide_dynamic-update-slice_fusion), channel_id=1, replica_groups=mesh['rx'=2,'rc'=2,'az'=4,'ay'=2] {'az'}, use_global_device_ids=true, to_apply=%add | all-reduce | flops 768 | bytes 6144
  284.3 0.4 collective-permute-start
  284.7 64.3 %collective-permute-done = f32[768]{0:T(1024)S(1)} collective-permute-done((f32[768]{0:T(1024)S(1)}, f32[768]{0:T(1024)S(1)}, u32[]{:S(2)}, u32[]{:S(2)}) %collective-permute-start) | collective-permute-done | bytes 3104 | tf_op jit(solution)/shard_map/ppermute | solution.py:31
  349.0 0.0 collective-permute-done.1
  349.0 0.0 collective-permute-done.2
  349.0 0.0 collective-permute-done.3
  349.0 0.0 collective-permute-done.4
  349.0 51.3 %maximum_maximum_fusion = bf16[1536,8192]{1,0:T(8,128)(2,1)} fusion(bf16[768,2048]{1,0:T(8,128)(2,1)} %collective-permute-done.4, bf16[768,2048]{1,0:T(8,128)(2,1)} %collective-permute-done.3, bf16[768,2048]{1,0:T(8,128)(2,1)} %collective-permute-done.2, bf16[768,2048]{1,0:T(8,128)(2,1)S(1)} %collective-permute-done.1, ...), kind=kLoop, calls=%fused_computation | loop fusion | flops 201326592 | bytes 50331648 | tf_op jit(solution)/shard_map/concatenate | solution.py:63
  400.4 34.6 %fusion = f32[1024,8192]{1,0:T(8,128)} fusion(bf16[1536,8192]{1,0:T(8,128)(2,1)} %maximum_maximum_fusion, s32[]{:T(128)S(6)} %select_n.43, f32[1536]{0:T(1024)S(1)} %pad_maximum_fusion), kind=kOutput, calls=%fused_computation.5 | convolution fusion | flops 25774522368 | bytes 61872132 | tf_op jit(solution)/shard_map/dot_general | solution.py:25
  434.9 42.6 %reshape.14 = f32[1024,2,2,2048]{3,2,1,0:T(2,128)} reshape(f32[1024,8192]{1,0:T(8,128)} %fusion) | data formatting | bytes 67108864 | tf_op jit(solution)/shard_map/reshape | solution.py:70
  477.5 41.3 %constant_dynamic-slice_fusion.1 = (f32[1024,2,1,2048]{3,2,1,0:T(1,128)}, f32[1024,2,1,2048]{3,2,1,0:T(1,128)}) fusion(f32[1024,2,2,2048]{3,2,1,0:T(2,128)} %reshape.14, s32[]{:T(128)S(6)} %select_n.44, s32[]{:T(128)S(6)} %select_n.45), kind=kLoop, calls=%fused_computation.16 | loop fusion | bytes 67108872 | tf_op jit(solution)/shard_map/dynamic_slice | solution.py:38
  518.8 15.7 %copy.12 = f32[1024,2,1,2048]{3,0,2,1:T(8,128)} copy(f32[1024,2,1,2048]{3,2,1,0:T(1,128)} %get-tuple-element.6) | data formatting | bytes 33554432
  534.5 0.0 collective-permute-start.5
  534.5 25.5 %collective-permute-done.5 = f32[1024,2,1,2048]{3,0,2,1:T(8,128)} collective-permute-done((f32[1024,2,1,2048]{3,0,2,1:T(8,128)}, f32[1024,2,1,2048]{3,0,2,1:T(8,128)}, u32[]{:S(2)}, u32[]{:S(2)}) %collective-permute-start.5) | collective-permute-done | bytes 16777248 | tf_op jit(solution)/shard_map/ppermute | solution.py:31
  560.0 14.5 %copy_add_fusion = f32[1024,2,1,2048]{3,0,2,1:T(8,128)S(1)} fusion(f32[1024,2,1,2048]{3,0,2,1:T(8,128)} %collective-permute-done.5, f32[1024,2,1,2048]{3,2,1,0:T(1,128)} %get-tuple-element.5), kind=kLoop, calls=%fused_computation.1 | loop fusion | flops 4194304 | bytes 50331648 | tf_op jit(solution)/shard_map/add | solution.py:41
  574.5 0.0 copy-start
  574.5 5.7 copy-done
  580.3 2.7 dynamic-slice_convert_fusion
  582.9 1.5 collective-permute-start.6
  584.4 91.5 %collective-permute-done.6 = bf16[1024,1,1,2048]{3,0,2,1:T(8,128)(2,1)} collective-permute-done((bf16[1024,1,1,2048]{3,0,2,1:T(8,128)(2,1)}, bf16[1024,1,1,2048]{3,0,2,1:T(8,128)(2,1)}, u32[]{:S(2)}, u32[]{:S(2)}) %collective-permute-start.6) | collective-permute-done | bytes 4194336 | tf_op jit(solution)/shard_map/ppermute | solution.py:31
  675.8 10.1 %add_bitcast_fusion = f32[1024,2048]{1,0:T(8,128)} fusion(bf16[1024,1,1,2048]{3,0,2,1:T(8,128)(2,1)} %collective-permute-done.6, f32[1024,2,1,2048]{3,0,2,1:T(8,128)} %copy-done, s32[]{:T(128)S(6)} %select_n.46), kind=kLoop, calls=%fused_computation.2 | loop fusion | flops 4194304 | bytes 20971524 | tf_op jit(solution)/shard_map/reshape | solution.py:73
  (2 shorter events, 0.0 us)
Async XLA Ops:
  6.5 70.0 %all-gather.5.cloned.1.call-start = ((), (), s32[]{:S(2)}) async-start(), calls=%async_computation | async-start | bytes 3932160 | tf_op jit(solution)/shard_map/all_gather | solution.py:55
  10.2 130.1 %all-gather.7.cloned.1.call-start = ((), (), s32[]{:S(2)}) async-start(), calls=%async_computation.1 | async-start | bytes 3932160 | tf_op jit(solution)/shard_map/all_gather | solution.py:55
  11.0 193.1 %all-gather.9.cloned.1.call-start = ((), (), s32[]{:S(2)}) async-start(), calls=%async_computation.2 | async-start | bytes 3932160 | tf_op jit(solution)/shard_map/all_gather | solution.py:55
  11.7 256.0 %all-gather.11.cloned.1.call-start = ((), (), s32[]{:S(2)}) async-start(), calls=%async_computation.3 | async-start | bytes 3932160 | tf_op jit(solution)/shard_map/all_gather | solution.py:55
  76.6 272.4 %collective-permute-start.1 = (bf16[768,2048]{1,0:T(8,128)(2,1)}, bf16[768,2048]{1,0:T(8,128)(2,1)S(1)}, u32[]{:S(2)}, u32[]{:S(2)}) collective-permute-start(bf16[768,2048]{1,0:T(8,128)(2,1)} %all-gather.5.cloned.1.call-done), channel_id=1, source_target_pairs={{0,1},{1,0},{2,3},{3,2},{4,5},{5,4},{6,7},{7,6},{8,9},{9,8},{10,11... | collective-permute-start | bytes 9437192 | tf_op jit(solution)/shard_map/ppermute | solution.py:31
  140.3 208.7 %collective-permute-start.2 = (bf16[768,2048]{1,0:T(8,128)(2,1)}, bf16[768,2048]{1,0:T(8,128)(2,1)}, u32[]{:S(2)}, u32[]{:S(2)}) collective-permute-start(bf16[768,2048]{1,0:T(8,128)(2,1)} %all-gather.7.cloned.1.call-done), channel_id=1, source_target_pairs={{0,1},{1,0},{2,3},{3,2},{4,5},{5,4},{6,7},{7,6},{8,9},{9,8},{10,11... | collective-permute-start | bytes 9437192 | tf_op jit(solution)/shard_map/ppermute | solution.py:31
  204.1 144.9 %collective-permute-start.3 = (bf16[768,2048]{1,0:T(8,128)(2,1)}, bf16[768,2048]{1,0:T(8,128)(2,1)}, u32[]{:S(2)}, u32[]{:S(2)}) collective-permute-start(bf16[768,2048]{1,0:T(8,128)(2,1)} %all-gather.9.cloned.1.call-done), channel_id=1, source_target_pairs={{0,1},{1,0},{2,3},{3,2},{4,5},{5,4},{6,7},{7,6},{8,9},{9,8},{10,11... | collective-permute-start | bytes 9437192 | tf_op jit(solution)/shard_map/ppermute | solution.py:31
  267.7 81.3 %collective-permute-start.4 = (bf16[768,2048]{1,0:T(8,128)(2,1)}, bf16[768,2048]{1,0:T(8,128)(2,1)}, u32[]{:S(2)}, u32[]{:S(2)}) collective-permute-start(bf16[768,2048]{1,0:T(8,128)(2,1)} %all-gather.11.cloned.1.call-done), channel_id=1, source_target_pairs={{0,1},{1,0},{2,3},{3,2},{4,5},{5,4},{6,7},{7,6},{8,9},{9,8},{10,11... | collective-permute-start | bytes 9437192 | tf_op jit(solution)/shard_map/ppermute | solution.py:31
  284.3 64.7 %collective-permute-start = (f32[768]{0:T(1024)S(1)}, f32[768]{0:T(1024)S(1)}, u32[]{:S(2)}, u32[]{:S(2)}) collective-permute-start(f32[768]{0:T(1024)S(1)} %all-reduce), channel_id=1, source_target_pairs={{0,1},{1,0},{2,3},{3,2},{4,5},{5,4},{6,7},{7,6},{8,9},{9,8},{10,11... | collective-permute-start | bytes 9224 | tf_op jit(solution)/shard_map/ppermute | solution.py:31
  534.5 25.5 %collective-permute-start.5 = (f32[1024,2,1,2048]{3,0,2,1:T(8,128)}, f32[1024,2,1,2048]{3,0,2,1:T(8,128)}, u32[]{:S(2)}, u32[]{:S(2)}) collective-permute-start(f32[1024,2,1,2048]{3,0,2,1:T(8,128)} %copy.12), channel_id=1, source_target_pairs={{0,8},{8,0},{1,9},{9,1},{2,10},{10,2},{3,11},{11,3},{4,12},{12,4},... | collective-permute-start | bytes 50331656 | tf_op jit(solution)/shard_map/ppermute | solution.py:31
  574.5 5.7 copy-start
  582.9 92.9 %collective-permute-start.6 = (bf16[1024,1,1,2048]{3,0,2,1:T(8,128)(2,1)}, bf16[1024,1,1,2048]{3,0,2,1:T(8,128)(2,1)}, u32[]{:S(2)}, u32[]{:S(2)}) collective-permute-start(bf16[1024,1,1,2048]{3,0,2,1:T(8,128)(2,1)} %dynamic-slice_convert_fusion), channel_id=1, source_target_pairs={{0,16},{16,0},{1,17},{17,1},{2,18},{18,2},{3,19},{19,3},{4,20},{20... | collective-permute-start | bytes 12582920 | tf_op jit(solution)/shard_map/ppermute | solution.py:31
Sparse Core Ops, SparseCore 0:
  10.3 66.1 all-gather.4
  78.1 62.1 all-gather.6
  141.9 62.1 all-gather.8
  205.5 62.1 all-gather.10

commit v3 on v1

v3 whole, which is shorter than its diff:
```python
import jax
import jax.numpy as jnp
from jax import lax
from jax.sharding import Mesh, PartitionSpec as P

NVIR = 1536
NOCC_B = 4


def row_weights(pairs, e_occ, e_vir, occ_batch, freq):
    batch_start = occ_batch[0] * NOCC_B
    e_batch = lax.dynamic_slice_in_dim(e_occ, batch_start, NOCC_B, 0)
    occ = pairs // NVIR
    vir = pairs % NVIR
    occ_hit = occ[:, None] == jnp.arange(NOCC_B, dtype=jnp.int32)[None, :]
    vir_hit = vir[:, None] == jnp.arange(e_vir.shape[0], dtype=jnp.int32)[None, :]
    e_low = jnp.sum(jnp.where(occ_hit, e_batch[None, :], 0.0), axis=1)
    e_high = jnp.sum(jnp.where(vir_hit, e_vir[None, :], 0.0), axis=1)
    delta = e_high - e_low
    return 2.0 * delta / (delta * delta + freq[0] * freq[0])


def contract(left, right):
    return lax.dot_general(
        left, right, (((0,), (0,)), ((), ())), preferred_element_type=jnp.float32
    )


def swap(x, axis):
    return lax.ppermute(x, axis, [(0, 1), (1, 0)])


def scale(weight, cols):
    return (weight[:, None] * cols.astype(jnp.float32)).astype(jnp.bfloat16)


def make_body(n_rx, n_rc, n_az, n_ay):
    def body(b_rows, pair_index, e_occ, e_vir, occ_batch, freq):
        nloc, naux = b_rows.shape
        width = naux // (n_az * n_ay)
        rw = naux // (n_rx * n_rc)
        z = lax.axis_index("az")
        x = lax.axis_index("rx")
        c = lax.axis_index("rc")
        a = z * n_ay + lax.axis_index("ay")
        order = [(1 - x) * 2 + (1 - c), x * 2 + (1 - c), (1 - x) * 2 + c, x * 2 + c]
        home = (a * width) // rw
        off = (a * width) % rw

        def others(v):
            doubled = jnp.concatenate([v, v], axis=0)
            return lax.dynamic_slice_in_dim(doubled, (z + 1) * nloc, (n_az - 1) * nloc, axis=0)

        def pick(blocks):
            out = lax.dynamic_slice_in_dim(blocks[0], off, width, axis=1)
            for k in range(1, len(blocks)):
                out = jnp.where(order[k] == home, lax.dynamic_slice_in_dim(blocks[k], off, width, axis=1), out)
            return out

        w_own = row_weights(pair_index, e_occ, e_vir, occ_batch, freq)
        w_a = swap(w_own, "ay")
        theirs_own = swap(b_rows, "ay")
        w_z = lax.all_gather(w_own, "az", axis=0, tiled=True)
        w_b = swap(others(w_z), "ay")
        mine, theirs = [], []
        for m in order:
            piece = lax.all_gather(
                lax.dynamic_slice_in_dim(b_rows, m * rw, rw, axis=1), "az", axis=0, tiled=True
            )
            mine.append(piece)
            theirs.append(swap(others(piece), "ay"))
        s_mine = scale(w_z, pick(mine))
        s_b = scale(w_b, pick(theirs))
        s_a = scale(w_a, lax.dynamic_slice_in_dim(theirs_own, a * width, width, axis=1))
        blocks = []
        for k, m in enumerate(order):
            cols_a = lax.dynamic_slice_in_dim(theirs_own, m * rw, rw, axis=1)
            blocks.append(contract(s_mine, mine[k]) + contract(s_b, theirs[k]) + contract(s_a, cols_a))
        got_other = swap(blocks[0], "rc")
        got_own = swap(blocks[1], "rc")
        other_x = blocks[2] + got_other
        got_x = swap(other_x.astype(jnp.bfloat16), "rx")
        return blocks[3] + got_own + got_x.astype(jnp.float32)

    return body


def make_plain_body(n_rows, n_aux):
    def body(b_rows, pair_index, e_occ, e_vir, occ_batch, freq):
        width = b_rows.shape[1] // n_aux
        group_pairs = lax.all_gather(pair_index, "aux", axis=0, tiled=True)
        group = lax.all_gather(b_rows, "aux", axis=0, tiled=True)
        own = lax.dynamic_slice_in_dim(group, lax.axis_index("aux") * width, width, axis=1)
        scaled = scale(row_weights(group_pairs, e_occ, e_vir, occ_batch, freq), own)
        return lax.psum_scatter(contract(scaled, group), "rows", scatter_dimension=1, tiled=True)

    return body


def solution(mesh):
    n_rows = mesh.shape["rows"]
    n_aux = mesh.shape["aux"]
    naux = 8192
    fits = n_rows == 4 and n_aux % 2 == 0 and (naux // n_rows) % (naux // n_aux) == 0
    if not fits:
        placed = (P(("rows", "aux"), None), P(("rows", "aux")), P(), P(), P(), P())
        return jax.shard_map(
            make_plain_body(n_rows, n_aux), mesh=mesh, in_specs=placed,
            out_specs=P("aux", "rows"), check_vma=False,
        )
    n_rx, n_rc, n_ay = 2, 2, 2
    n_az = n_aux // n_ay
    split = Mesh(mesh.devices.reshape(n_rx, n_rc, n_az, n_ay), ("rx", "rc", "az", "ay"))
    rows_all = ("rx", "rc", "az", "ay")
    placed = (P(rows_all, None), P(rows_all), P(), P(), P(), P())
    return jax.shard_map(
        make_body(n_rx, n_rc, n_az, n_ay),
        mesh=split,
        in_specs=placed,
        out_specs=P(("az", "ay"), ("rx", "rc")),
        check_vma=False,
    )
```

time: 887 us -> 574 us (0.65)
  waiting for transfers between devices: 793 us -> 399 us
  other arithmetic: 0.51 us -> 54 us
  matrix products: 33.8 us -> 72.3 us
  local copies, waits for them, and re-layouts: 31.4 us -> 5.02 us
  starting transfers between devices: 0.13 us -> 10.6 us
    all_gather x2 -> x4, waiting for transfers between devices: 500 us -> 219 us  [body(): lax.all_gather(lax.dynamic_slice_in_dim(b_rows, m * rw, rw, axis=1), 'az'...]
    reduce_scatter x1 -> x0, waiting for transfers between devices: 191 us -> none  [body(): lax.psum_scatter(partial_value, 'rx', scatter_dimension=1, tiled=True)]
    ppermute x0 -> x10, waiting for transfers between devices: none -> 178 us  [swap(): return lax.ppermute(x, axis, [(0, 1), (1, 0)])]
    unnamed x5 -> x4, waiting for transfers between devices: 102 us -> 1.92 us
    dot_general x1 -> x12, matrix products: 33.8 us -> 72.3 us  [contract(): lax.dot_general(left, right, (((0,), (0,)), ((), ())), preferred_element_...]
    concatenate x0 -> x5, other arithmetic: none -> 20.1 us  [others(): doubled = jnp.concatenate([v, v], axis=0)]
    convert_element_type x0 -> x3, other arithmetic: none -> 18.2 us  [the longest x1 11.8 us: body(): got_x = swap(other_x.astype(jnp.bfloat16), 'rx')]
    all_gather x1 -> x0, local copies, waits for them, and re-layouts: 16.6 us -> none  [body(): group = lax.all_gather(b_rows, 'az', axis=0, tiled=True)]
  transfers between devices with their start and end apart: 4 -> 14, of which waited for: 4 -> 7; matrix products, arithmetic and copies ran while one was open for 0% -> 19% of each run, Pallas kernels for 0% -> 0%
where the time goes in v3:
time: 574 us; the launch traced here: 570 us
  waiting for transfers between devices  399 us (70%)
  matrix products  72.3 us (13%)
  other arithmetic  54 us (9%)
  between operations  15.4 us (3%)
  blocking collectives  13.7 us (2%)
  starting transfers between devices  10.6 us (2%)
    all_gather x4, waiting for transfers between devices, body(): lax.all_gather(lax.dynamic_slice_in_dim(b_rows, m * rw, rw, axis=1), 'az'...  219 us
    ppermute x10, waiting for transfers between devices, swap(): return lax.ppermute(x, axis, [(0, 1), (1, 0)])  178 us
    dot_general x12, matrix products, contract(): lax.dot_general(left, right, (((0,), (0,)), ((), ())), preferred_element_...  72.3 us
    concatenate x5, other arithmetic, others(): doubled = jnp.concatenate([v, v], axis=0)  20.1 us
    add x1, other arithmetic, body(): return blocks[3] + got_own + got_x.astype(jnp.float32)  15.2 us
    unnamed x1, blocking collectives  13.7 us
    convert_element_type x1, other arithmetic, body(): got_x = swap(other_x.astype(jnp.bfloat16), 'rx')  11.8 us
  transfers between devices with their start and end apart: 14, of which 7 were waited for; matrix products, arithmetic and copies ran while one was open for 19% of the time, Pallas kernels for 0%

profile of v3, /device:TPU:0, one launch (start us, length us, event | category | flops | bytes accessed | tf_op | source)
XLA Modules:
  0.0 569.8 jit_solution(12427656286531128736)
XLA Ops:
  6.5 3.7 constant_dynamic-slice_fusion.3
  10.2 0.0 all-gather.7.cloned.1.call-start
  10.3 0.7 all-gather.7.cloned.1.call-update
  11.0 0.7 all-gather.9.cloned.1.call-update
  11.8 0.5 all-gather.11.cloned.1.call-update
  13.6 0.8 dynamic_slice.69
  14.4 0.6 dynamic-slice
  15.5 0.1 select_reduce_fusion.1
  15.6 0.3 select_reduce_fusion
  15.9 0.1 fusion.15
  16.0 13.7 %all-reduce = f32[768]{0:T(1024)S(1)} all-reduce(f32[768]{0:T(1024)S(1)} %get-tuple-element.5), channel_id=1, replica_groups=mesh['rx'=2,'rc'=2,'az'=4,'ay'=2] {'az'}, use_global_device_ids=true, to_apply=%add | all-reduce | flops 768 | bytes 6144
  29.7 46.9 %all-gather.5.cloned.1.call-done = bf16[768,2048]{1,0:T(8,128)(2,1)} async-done(((bf16[192,2048]{1,0:T(8,128)(2,1)}), bf16[768,2048]{1,0:T(8,128)(2,1)}) %all-gather.5.cloned.1.call-update) | async-done | bytes 3145744 | tf_op jit(solution)/shard_map/all_gather | solution.py:67
  76.6 5.0 fusion.3
  81.6 1.5 collective-permute-start.1
  83.1 57.3 %all-gather.7.cloned.1.call-done = bf16[768,2048]{1,0:T(8,128)(2,1)} async-done(((bf16[192,2048]{1,0:T(8,128)(2,1)}), bf16[768,2048]{1,0:T(8,128)(2,1)}) %all-gather.7.cloned.1.call-update) | async-done | bytes 3145744 | tf_op jit(solution)/shard_map/all_gather | solution.py:67
  140.4 5.0 fusion.2
  145.4 1.5 collective-permute-start.2
  146.9 57.2 %all-gather.9.cloned.1.call-done = bf16[768,2048]{1,0:T(8,128)(2,1)} async-done(((bf16[192,2048]{1,0:T(8,128)(2,1)}), bf16[768,2048]{1,0:T(8,128)(2,1)}) %all-gather.9.cloned.1.call-update) | async-done | bytes 3145744 | tf_op jit(solution)/shard_map/all_gather | solution.py:67
  204.1 5.0 fusion.1
  209.1 1.5 collective-permute-start.3
  210.6 57.1 %all-gather.11.cloned.1.call-done = bf16[768,2048]{1,0:T(8,128)(2,1)} async-done(((bf16[192,2048]{1,0:T(8,128)(2,1)}), bf16[768,2048]{1,0:T(8,128)(2,1)}) %all-gather.11.cloned.1.call-update) | async-done | bytes 3145744 | tf_op jit(solution)/shard_map/all_gather | solution.py:67
  267.7 5.0 fusion
  272.7 1.5 collective-permute-start.4
  274.2 0.1 fusion.14
  274.3 0.6 collective-permute-start
  274.9 51.2 %collective-permute-done = f32[576]{0:T(1024)S(1)} collective-permute-done((f32[576]{0:T(1024)S(1)}, f32[576]{0:T(1024)S(1)}, u32[]{:S(2)}, u32[]{:S(2)}) %collective-permute-start) | collective-permute-done | bytes 2336 | tf_op jit(solution)/shard_map/ppermute | solution.py:30
  326.1 1.5 collective-permute-start.6
  327.5 3.4 multiply_convert_fusion
  330.9 3.9 fusion.22
  334.8 0.6 collective-permute-start.5
  335.4 3.0 multiply_convert_fusion.1
  338.4 5.2 fusion.23
  343.6 51.7 %collective-permute-done.5 = f32[192]{0:T(256)S(1)} collective-permute-done((f32[192]{0:T(256)S(1)}, f32[192]{0:T(256)S(1)}, u32[]{:S(2)}, u32[]{:S(2)}) %collective-permute-start.5) | collective-permute-done | bytes 800 | tf_op jit(solution)/shard_map/ppermute | solution.py:30
  395.4 6.1 %add_add_fusion = f32[1024,2048]{1,0:T(8,128)} fusion(f32[1024,2048]{1,0:T(8,128)S(1)} %fusion.22, f32[1024,2048]{1,0:T(8,128)S(1)} %fusion.23, bf16[192,8192]{1,0:T(8,128)(2,1)} %collective-permute-done.6, s32[]{:T(128)S(6)} %select_n.123, s32[]{:T(128)S(6)} %select_n.134, f32[192]{0:T(256)S(1)} %collective-permute-done.5), kind=kOutput, calls=%fused_computation.2 | convolution fusion | flops 810090496 | bytes 26346248 | tf_op jit(solution)/shard_map/dot_general | solution.py:24
  401.5 3.5 fusion.18
  405.0 15.8 %fusion.19 = f32[1024,2048]{1,0:T(8,128)S(1)} fusion(bf16[576,1024]{1,0:T(8,128)(2,1)S(1)} %multiply_convert_fusion.1, bf16[576,2048]{1,0:T(8,128)(2,1)} %collective-permute-done.3), kind=kOutput, calls=%fused_computation.48 | convolution fusion | flops 2415919104 | bytes 11927552 | tf_op jit(solution)/shard_map/dot_general | solution.py:24
  420.8 6.0 %add_add_fusion.1 = f32[1024,2048]{1,0:T(8,128)} fusion(f32[1024,2048]{1,0:T(8,128)S(1)} %fusion.18, f32[1024,2048]{1,0:T(8,128)S(1)} %fusion.19, bf16[192,8192]{1,0:T(8,128)(2,1)} %collective-permute-done.6, s32[]{:T(128)S(6)} %select_n.122, s32[]{:T(128)S(6)} %select_n.134, f32[192]{0:T(256)S(1)} %collective-permute-done.5), kind=kOutput, calls=%fused_computation.3 | convolution fusion | flops 810090496 | bytes 26346248 | tf_op jit(solution)/shard_map/dot_general | solution.py:24
  426.7 0.5 collective-permute-start.7
  427.2 2.9 fusion.5
  430.1 5.8 %fusion.20 = f32[1024,2048]{1,0:T(8,128)} fusion(bf16[768,1024]{1,0:T(8,128)(2,1)S(1)} %multiply_convert_fusion, bf16[768,2048]{1,0:T(8,128)(2,1)S(1)} %copy-done.2), kind=kOutput, calls=%fused_computation.49 | convolution fusion | flops 3221225472 | bytes 13107200 | tf_op jit(solution)/shard_map/dot_general | solution.py:24
  436.0 7.4 %fusion.21 = f32[1024,2048]{1,0:T(8,128)} fusion(bf16[576,1024]{1,0:T(8,128)(2,1)S(1)} %multiply_convert_fusion.1, bf16[576,2048]{1,0:T(8,128)(2,1)} %collective-permute-done.2), kind=kOutput, calls=%fused_computation.50 | convolution fusion | flops 2415919104 | bytes 11927552 | tf_op jit(solution)/shard_map/dot_general | solution.py:24
  443.3 11.8 %add_convert_fusion = bf16[1024,2048]{1,0:T(8,128)(2,1)} fusion(f32[1024,2048]{1,0:T(8,128)} %collective-permute-done.8, f32[1024,2048]{1,0:T(8,128)S(1)} %fusion.5, f32[1024,2048]{1,0:T(8,128)} %fusion.20, f32[1024,2048]{1,0:T(8,128)} %fusion.21), kind=kLoop, calls=%fused_computation.1 | loop fusion | flops 8388608 | bytes 37748736 | tf_op jit(solution)/shard_map/convert_element_type | solution.py:82
  455.2 1.5 collective-permute-start.9
  456.6 2.6 fusion.8
  459.3 5.7 %fusion.16 = f32[1024,2048]{1,0:T(8,128)} fusion(bf16[768,1024]{1,0:T(8,128)(2,1)S(1)} %copy-done.6, bf16[768,2048]{1,0:T(8,128)(2,1)S(1)} %copy-done.1), kind=kOutput, calls=%fused_computation.45 | convolution fusion | flops 3221225472 | bytes 13107200 | tf_op jit(solution)/shard_map/dot_general | solution.py:24
  465.1 7.4 %fusion.17 = f32[1024,2048]{1,0:T(8,128)} fusion(bf16[576,1024]{1,0:T(8,128)(2,1)S(1)} %multiply_convert_fusion.1, bf16[576,2048]{1,0:T(8,128)(2,1)} %collective-permute-done.1), kind=kOutput, calls=%fused_computation.46 | convolution fusion | flops 2415919104 | bytes 11927552 | tf_op jit(solution)/shard_map/dot_general | solution.py:24
  472.5 75.4 %collective-permute-done.9 = bf16[1024,2048]{1,0:T(8,128)(2,1)} collective-permute-done((bf16[1024,2048]{1,0:T(8,128)(2,1)}, bf16[1024,2048]{1,0:T(8,128)(2,1)}, u32[]{:S(2)}, u32[]{:S(2)}) %collective-permute-start.9) | collective-permute-done | bytes 4194336 | tf_op jit(solution)/shard_map/ppermute | solution.py:30
  547.9 15.2 %convert_add_fusion = f32[1024,2048]{1,0:T(8,128)} fusion(bf16[1024,2048]{1,0:T(8,128)(2,1)} %collective-permute-done.9, f32[1024,2048]{1,0:T(8,128)} %collective-permute-done.7, f32[1024,2048]{1,0:T(8,128)S(1)} %fusion.8, f32[1024,2048]{1,0:T(8,128)} %fusion.16, f32[1024,2048]{1,0:T(8,128)} %fusion.17), kind=kLoop, calls=%fused_computation | loop fusion | flops 10485760 | bytes 46137344 | tf_op jit(solution)/shard_map/add | solution.py:83
  (34 shorter events, 0.2 us)
Async XLA Ops:
  6.5 70.1 %all-gather.5.cloned.1.call-start = ((), (), s32[]{:S(2)}) async-start(), calls=%async_computation | async-start | bytes 3932160 | tf_op jit(solution)/shard_map/all_gather | solution.py:67
  10.2 4.2 copy-start.9
  10.2 5.3 copy-start.8
  10.2 5.4 copy-start.7
  10.2 130.2 %all-gather.7.cloned.1.call-start = ((), (), s32[]{:S(2)}) async-start(), calls=%async_computation.1 | async-start | bytes 3932160 | tf_op jit(solution)/shard_map/all_gather | solution.py:67
  11.0 193.2 %all-gather.9.cloned.1.call-start = ((), (), s32[]{:S(2)}) async-start(), calls=%async_computation.2 | async-start | bytes 3932160 | tf_op jit(solution)/shard_map/all_gather | solution.py:67
  11.7 256.0 %all-gather.11.cloned.1.call-start = ((), (), s32[]{:S(2)}) async-start(), calls=%async_computation.3 | async-start | bytes 3932160 | tf_op jit(solution)/shard_map/all_gather | solution.py:67
  81.6 253.2 %collective-permute-start.1 = (bf16[576,2048]{1,0:T(8,128)(2,1)}, bf16[576,2048]{1,0:T(8,128)(2,1)}, u32[]{:S(2)}, u32[]{:S(2)}) collective-permute-start(bf16[576,2048]{1,0:T(8,128)(2,1)} %fusion.3), channel_id=1, source_target_pairs={{0,1},{1,0},{2,3},{3,2},{4,5},{5,4},{6,7},{7,6},{8,9},{9,8},{10,11... | collective-permute-start | bytes 7077896 | tf_op jit(solution)/shard_map/ppermute | solution.py:30
  145.4 190.0 %collective-permute-start.2 = (bf16[576,2048]{1,0:T(8,128)(2,1)}, bf16[576,2048]{1,0:T(8,128)(2,1)}, u32[]{:S(2)}, u32[]{:S(2)}) collective-permute-start(bf16[576,2048]{1,0:T(8,128)(2,1)} %fusion.2), channel_id=1, source_target_pairs={{0,1},{1,0},{2,3},{3,2},{4,5},{5,4},{6,7},{7,6},{8,9},{9,8},{10,11... | collective-permute-start | bytes 7077896 | tf_op jit(solution)/shard_map/ppermute | solution.py:30
  209.1 118.4 %copy-start = (bf16[768,2048]{1,0:T(8,128)(2,1)S(1)}, bf16[768,2048]{1,0:T(8,128)(2,1)}, u32[]{:S(2)}) copy-start(bf16[768,2048]{1,0:T(8,128)(2,1)} %all-gather.5.cloned.1.call-done) | copy-start | bytes 9437188
  209.1 126.3 %collective-permute-start.3 = (bf16[576,2048]{1,0:T(8,128)(2,1)}, bf16[576,2048]{1,0:T(8,128)(2,1)}, u32[]{:S(2)}, u32[]{:S(2)}) collective-permute-start(bf16[576,2048]{1,0:T(8,128)(2,1)} %fusion.1), channel_id=1, source_target_pairs={{0,1},{1,0},{2,3},{3,2},{4,5},{5,4},{6,7},{7,6},{8,9},{9,8},{10,11... | collective-permute-start | bytes 7077896 | tf_op jit(solution)/shard_map/ppermute | solution.py:30
  272.7 62.7 %collective-permute-start.4 = (bf16[576,2048]{1,0:T(8,128)(2,1)}, bf16[576,2048]{1,0:T(8,128)(2,1)}, u32[]{:S(2)}, u32[]{:S(2)}) collective-permute-start(bf16[576,2048]{1,0:T(8,128)(2,1)} %fusion), channel_id=1, source_target_pairs={{0,1},{1,0},{2,3},{3,2},{4,5},{5,4},{6,7},{7,6},{8,9},{9,8},{10,11... | collective-permute-start | bytes 7077896 | tf_op jit(solution)/shard_map/ppermute | solution.py:30
  274.3 51.8 %collective-permute-start = (f32[576]{0:T(1024)S(1)}, f32[576]{0:T(1024)S(1)}, u32[]{:S(2)}, u32[]{:S(2)}) collective-permute-start(f32[576]{0:T(1024)S(1)} %fusion.14), channel_id=1, source_target_pairs={{0,1},{1,0},{2,3},{3,2},{4,5},{5,4},{6,7},{7,6},{8,9},{9,8},{10,11... | collective-permute-start | bytes 6920 | tf_op jit(solution)/shard_map/ppermute | solution.py:30
  326.1 69.3 %collective-permute-start.6 = (bf16[192,8192]{1,0:T(8,128)(2,1)}, bf16[192,8192]{1,0:T(8,128)(2,1)}, u32[]{:S(2)}, u32[]{:S(2)}) collective-permute-start(bf16[192,8192]{1,0:T(8,128)(2,1)} %param.6), channel_id=1, source_target_pairs={{0,1},{1,0},{2,3},{3,2},{4,5},{5,4},{6,7},{7,6},{8,9},{9,8},{10,11... | collective-permute-start | bytes 9437192 | tf_op jit(solution)/shard_map/ppermute | solution.py:30
  327.5 3.4 copy-start.4
  330.9 99.2 %copy-start.5 = (bf16[768,1024]{1,0:T(8,128)(2,1)}, bf16[768,1024]{1,0:T(8,128)(2,1)S(1)}, u32[]{:S(2)}) copy-start(bf16[768,1024]{1,0:T(8,128)(2,1)S(1)} %multiply_convert_fusion) | copy-start | bytes 4718596
  334.8 60.5 %collective-permute-start.5 = (f32[192]{0:T(256)S(1)}, f32[192]{0:T(256)S(1)}, u32[]{:S(2)}, u32[]{:S(2)}) collective-permute-start(f32[192]{0:T(256)S(1)} %get-tuple-element.6), channel_id=1, source_target_pairs={{0,1},{1,0},{2,3},{3,2},{4,5},{5,4},{6,7},{7,6},{8,9},{9,8},{10,11... | collective-permute-start | bytes 2312 | tf_op jit(solution)/shard_map/ppermute | solution.py:30
  343.6 57.8 %copy-start.3 = (bf16[768,2048]{1,0:T(8,128)(2,1)S(1)}, bf16[768,2048]{1,0:T(8,128)(2,1)}, u32[]{:S(2)}) copy-start(bf16[768,2048]{1,0:T(8,128)(2,1)} %all-gather.9.cloned.1.call-done) | copy-start | bytes 9437188
  401.5 41.9 %collective-permute-start.8 = (f32[1024,2048]{1,0:T(8,128)}, f32[1024,2048]{1,0:T(8,128)}, u32[]{:S(2)}, u32[]{:S(2)}) collective-permute-start(f32[1024,2048]{1,0:T(8,128)} %add_add_fusion), channel_id=1, source_target_pairs={{0,8},{8,0},{1,9},{9,1},{2,10},{10,2},{3,11},{11,3},{4,12},{12,4},... | collective-permute-start | bytes 25165832 | tf_op jit(solution)/shard_map/ppermute | solution.py:30
  426.7 3.4 copy-start.2
  426.7 45.8 %collective-permute-start.7 = (f32[1024,2048]{1,0:T(8,128)}, f32[1024,2048]{1,0:T(8,128)}, u32[]{:S(2)}, u32[]{:S(2)}) collective-permute-start(f32[1024,2048]{1,0:T(8,128)} %add_add_fusion.1), channel_id=1, source_target_pairs={{0,8},{8,0},{1,9},{9,1},{2,10},{10,2},{3,11},{11,3},{4,12},{12,4},... | collective-permute-start | bytes 25165832 | tf_op jit(solution)/shard_map/ppermute | solution.py:30
  455.2 4.1 copy-start.1
  455.2 4.1 copy-start.6
  455.2 92.7 %collective-permute-start.9 = (bf16[1024,2048]{1,0:T(8,128)(2,1)}, bf16[1024,2048]{1,0:T(8,128)(2,1)}, u32[]{:S(2)}, u32[]{:S(2)}) collective-permute-start(bf16[1024,2048]{1,0:T(8,128)(2,1)} %add_convert_fusion), channel_id=1, source_target_pairs={{0,16},{16,0},{1,17},{17,1},{2,18},{18,2},{3,19},{19,3},{4,20},{20... | collective-permute-start | bytes 12582920 | tf_op jit(solution)/shard_map/ppermute | solution.py:30
Sparse Core Ops, SparseCore 0:
  10.3 66.2 all-gather.4
  78.2 62.1 all-gather.6
  141.9 62.1 all-gather.8
  205.6 62.1 all-gather.10

commit v4 on v3

--- a/solution.py
+++ b/solution.py
@@ -58,29 +58,34 @@
             return out
 
         w_own = row_weights(pair_index, e_occ, e_vir, occ_batch, freq)
+        w_z = lax.all_gather(w_own, "az", axis=0, tiled=True)
+        first = lax.dynamic_slice_in_dim(b_rows, order[0] * rw, rw, axis=1)
+        mine = [lax.all_gather(first, "az", axis=0, tiled=True)]
         w_a = swap(w_own, "ay")
+        w_b = swap(others(w_z), "ay")
         theirs_own = swap(b_rows, "ay")
-        w_z = lax.all_gather(w_own, "az", axis=0, tiled=True)
-        w_b = swap(others(w_z), "ay")
-        mine, theirs = [], []
-        for m in order:
+        theirs_own, w_a, w_b, rest = lax.optimization_barrier((theirs_own, w_a, w_b, b_rows))
+        theirs = [swap(others(mine[0]), "ay")]
+        for m in order[1:]:
             piece = lax.all_gather(
-                lax.dynamic_slice_in_dim(b_rows, m * rw, rw, axis=1), "az", axis=0, tiled=True
+                lax.dynamic_slice_in_dim(rest, m * rw, rw, axis=1), "az", axis=0, tiled=True
             )
             mine.append(piece)
             theirs.append(swap(others(piece), "ay"))
         s_mine = scale(w_z, pick(mine))
-        s_b = scale(w_b, pick(theirs))
         s_a = scale(w_a, lax.dynamic_slice_in_dim(theirs_own, a * width, width, axis=1))
-        blocks = []
+        early = []
         for k, m in enumerate(order):
             cols_a = lax.dynamic_slice_in_dim(theirs_own, m * rw, rw, axis=1)
-            blocks.append(contract(s_mine, mine[k]) + contract(s_b, theirs[k]) + contract(s_a, cols_a))
+            early.append(contract(s_a, cols_a) + contract(s_mine, mine[k]))
+        s_b = scale(w_b, pick(theirs))
+        blocks = [early[k] + contract(s_b, theirs[k]) for k in range(len(order))]
         got_other = swap(blocks[0], "rc")
-        got_own = swap(blocks[1], "rc")
         other_x = blocks[2] + got_other
         got_x = swap(other_x.astype(jnp.bfloat16), "rx")
-        return blocks[3] + got_own + got_x.astype(jnp.float32)
+        got_own = swap(blocks[1], "rc")
+        own_x = lax.optimization_barrier(blocks[3] + got_own)
+        return own_x + got_x.astype(jnp.float32)
 
     return body
 

time: 574 us -> 505 us (0.88); the launches traced: 570 us -> 495 us
  waiting for transfers between devices: 399 us -> 325 us
  matrix products: 72.3 us -> 54.2 us
  other arithmetic: 54 us -> 62.9 us
  local copies, waits for them, and re-layouts: 5.02 us -> 11.6 us
    all_gather x4, waiting for transfers between devices: 219 us -> 171 us  [the longest x3 171 us: body(): lax.all_gather(lax.dynamic_slice_in_dim(rest, m * rw, rw, axis=1), 'az',...]
    ppermute x10, waiting for transfers between devices: 178 us -> 153 us  [swap(): return lax.ppermute(x, axis, [(0, 1), (1, 0)])]
    dot_general x12, matrix products: 72.3 us -> 54.2 us  [contract(): lax.dot_general(left, right, (((0,), (0,)), ((), ())), preferred_element_...]
    add x1 -> x2, other arithmetic: 15.2 us -> 23.7 us  [the longest x1 13.6 us: body(): own_x = lax.optimization_barrier(blocks[3] + got_own)]
  transfers between devices with their start and end apart: 14 -> 14, of which waited for: 7 -> 6; matrix products, arithmetic and copies ran while one was open for 19% -> 21% of each run, Pallas kernels for 0% -> 0%
where the time goes in v4:
time: 505 us; the launch traced here: 495 us
  waiting for transfers between devices  325 us (64%)
  other arithmetic  62.9 us (12%)
  matrix products  54.2 us (11%)
  between operations  15.4 us (3%)
  starting transfers between devices  12.8 us (3%)
  blocking collectives  12.3 us (2%)
  local copies, waits for them, and re-layouts  11.6 us (2%)
    all_gather x3, waiting for transfers between devices, body(): lax.all_gather(lax.dynamic_slice_in_dim(rest, m * rw, rw, axis=1), 'az',...  171 us
    ppermute x10, waiting for transfers between devices, swap(): return lax.ppermute(x, axis, [(0, 1), (1, 0)])  153 us
    dot_general x12, matrix products, contract(): lax.dot_general(left, right, (((0,), (0,)), ((), ())), preferred_element_...  54.2 us
    concatenate x5, other arithmetic, others(): doubled = jnp.concatenate([v, v], axis=0)  20.3 us
    add x1, other arithmetic, body(): own_x = lax.optimization_barrier(blocks[3] + got_own)  13.6 us
    ppermute x10, starting transfers between devices, swap(): return lax.ppermute(x, axis, [(0, 1), (1, 0)])  12.7 us
    unnamed x1, blocking collectives  12.3 us
    convert_element_type x1, other arithmetic, body(): got_x = swap(other_x.astype(jnp.bfloat16), 'rx')  11.8 us
  transfers between devices with their start and end apart: 14, of which 6 were waited for; matrix products, arithmetic and copies ran while one was open for 21% of the time, Pallas kernels for 0%

profile of v4, /device:TPU:0, one launch (start us, length us, event | category | flops | bytes accessed | tf_op | source)
XLA Modules:
  0.0 494.7 jit_solution(7207662552665862482)
XLA Ops:
  6.5 2.1 constant_dynamic-slice_fusion
  8.7 3.0 collective-permute-start
  13.0 1.3 dynamic-slice
  15.0 0.8 dynamic_slice.69
  15.7 0.7 and_select_fusion
  16.5 1.0 select_reduce_fusion
  17.6 12.3 %all-reduce = f32[768]{0:T(1024)S(1)} all-reduce(f32[768]{0:T(1024)S(1)} %get-tuple-element.13), channel_id=1, replica_groups=mesh['rx'=2,'rc'=2,'az'=4,'ay'=2] {'az'}, use_global_device_ids=true, to_apply=%add | all-reduce | flops 768 | bytes 6144
  30.4 1.6 collective-permute-start.1
  32.0 48.2 %collective-permute-done.1 = f32[192]{0:T(256)S(1)} collective-permute-done((f32[192]{0:T(256)S(1)}, f32[192]{0:T(256)S(1)}, u32[]{:S(2)}, u32[]{:S(2)}) %collective-permute-start.1) | collective-permute-done | bytes 800 | tf_op jit(solution)/shard_map/ppermute | solution.py:30
  80.2 3.1 constant_dynamic-slice_fusion.3
  83.4 0.7 all-gather.7.cloned.1.call-update
  84.1 0.5 all-gather.5.cloned.1.call-update
  84.7 5.0 %fusion = bf16[576,2048]{1,0:T(8,128)(2,1)} fusion(s32[]{:T(128)S(6)} %select_n.114, bf16[768,2048]{1,0:T(8,128)(2,1)} %all-gather.11.cloned.1.call-done), kind=kLoop, calls=%fused_computation.14 | loop fusion | flops 4718592 | bytes 5505028 | tf_op jit(solution)/shard_map/concatenate | solution.py:51
  89.7 1.7 collective-permute-start.6
  91.4 57.0 %all-gather.9.cloned.1.call-done = bf16[768,2048]{1,0:T(8,128)(2,1)} async-done(((bf16[192,2048]{1,0:T(8,128)(2,1)}), bf16[768,2048]{1,0:T(8,128)(2,1)}) %all-gather.9.cloned.1.call-update) | async-done | bytes 3145744 | tf_op jit(solution)/shard_map/all_gather | solution.py:70
  148.4 5.0 %fusion.1 = bf16[576,2048]{1,0:T(8,128)(2,1)} fusion(s32[]{:T(128)S(6)} %select_n.114, bf16[768,2048]{1,0:T(8,128)(2,1)} %all-gather.9.cloned.1.call-done), kind=kLoop, calls=%fused_computation.15 | loop fusion | flops 4718592 | bytes 5505028 | tf_op jit(solution)/shard_map/concatenate | solution.py:51
  153.5 1.5 collective-permute-start.5
  155.0 57.2 %all-gather.7.cloned.1.call-done = bf16[768,2048]{1,0:T(8,128)(2,1)} async-done(((bf16[192,2048]{1,0:T(8,128)(2,1)}), bf16[768,2048]{1,0:T(8,128)(2,1)}) %all-gather.7.cloned.1.call-update) | async-done | bytes 3145744 | tf_op jit(solution)/shard_map/all_gather | solution.py:70
  212.2 5.0 %fusion.2 = bf16[576,2048]{1,0:T(8,128)(2,1)} fusion(s32[]{:T(128)S(6)} %select_n.114, bf16[768,2048]{1,0:T(8,128)(2,1)} %all-gather.7.cloned.1.call-done), kind=kLoop, calls=%fused_computation.16 | loop fusion | flops 4718592 | bytes 5505028 | tf_op jit(solution)/shard_map/concatenate | solution.py:51
  217.2 1.5 collective-permute-start.4
  218.7 57.1 %all-gather.5.cloned.1.call-done = bf16[768,2048]{1,0:T(8,128)(2,1)} async-done(((bf16[192,2048]{1,0:T(8,128)(2,1)}), bf16[768,2048]{1,0:T(8,128)(2,1)}) %all-gather.5.cloned.1.call-update) | async-done | bytes 3145744 | tf_op jit(solution)/shard_map/all_gather | solution.py:70
  275.8 5.1 %fusion.3 = bf16[576,2048]{1,0:T(8,128)(2,1)} fusion(s32[]{:T(128)S(6)} %select_n.114, bf16[768,2048]{1,0:T(8,128)(2,1)} %all-gather.5.cloned.1.call-done), kind=kLoop, calls=%fused_computation.17 | loop fusion | flops 4718592 | bytes 5505028 | tf_op jit(solution)/shard_map/concatenate | solution.py:51
  280.9 1.5 collective-permute-start.3
  282.4 1.4 fusion.4
  283.8 0.5 copy-done
  284.3 1.0 copy-done.1
  285.2 0.9 copy-done.3
  286.1 2.3 multiply_convert_fusion
  288.5 3.8 fusion.23
  292.4 41.8 %collective-permute-done.3 = bf16[576,2048]{1,0:T(8,128)(2,1)} collective-permute-done((bf16[576,2048]{1,0:T(8,128)(2,1)}, bf16[576,2048]{1,0:T(8,128)(2,1)}, u32[]{:S(2)}, u32[]{:S(2)}) %collective-permute-start.3) | collective-permute-done | bytes 2359328 | tf_op jit(solution)/shard_map/ppermute | solution.py:30
  334.2 3.0 multiply_convert_fusion.1
  337.2 7.4 %add_add_fusion = f32[1024,2048]{1,0:T(8,128)} fusion(f32[1024,2048]{1,0:T(8,128)S(1)} %fusion.4, f32[1024,2048]{1,0:T(8,128)S(1)} %fusion.23, bf16[576,1024]{1,0:T(8,128)(2,1)S(1)} %multiply_convert_fusion.1, bf16[576,2048]{1,0:T(8,128)(2,1)} %collective-permute-done.6), kind=kOutput, calls=%fused_computation.2 | convolution fusion | flops 2420113408 | bytes 28704768 | tf_op jit(solution)/shard_map/dot_general | solution.py:24
  344.6 1.4 fusion.8
  346.0 0.5 copy-done.5
  347.0 3.5 fusion.20
  350.5 7.5 %add_add_fusion.1 = f32[1024,2048]{1,0:T(8,128)} fusion(f32[1024,2048]{1,0:T(8,128)S(1)} %fusion.8, f32[1024,2048]{1,0:T(8,128)S(1)} %fusion.20, bf16[576,1024]{1,0:T(8,128)(2,1)S(1)} %multiply_convert_fusion.1, bf16[576,2048]{1,0:T(8,128)(2,1)} %collective-permute-done.5), kind=kOutput, calls=%fused_computation.3 | convolution fusion | flops 2420113408 | bytes 28704768 | tf_op jit(solution)/shard_map/dot_general | solution.py:24
  358.0 1.4 fusion.6
  359.4 0.5 copy-done.4
  360.4 5.8 %fusion.21 = f32[1024,2048]{1,0:T(8,128)} fusion(bf16[768,1024]{1,0:T(8,128)(2,1)S(1)} %copy-done.8, bf16[768,2048]{1,0:T(8,128)(2,1)S(1)} %copy-done.4), kind=kOutput, calls=%fused_computation.51 | convolution fusion | flops 3221225472 | bytes 13107200 | tf_op jit(solution)/shard_map/dot_general | solution.py:24
  366.2 7.5 %fusion.22 = f32[1024,2048]{1,0:T(8,128)} fusion(bf16[576,1024]{1,0:T(8,128)(2,1)S(1)} %multiply_convert_fusion.1, bf16[576,2048]{1,0:T(8,128)(2,1)} %collective-permute-done.4), kind=kOutput, calls=%fused_computation.52 | convolution fusion | flops 2415919104 | bytes 11927552 | tf_op jit(solution)/shard_map/dot_general | solution.py:24
  373.7 11.8 %add_convert_fusion = bf16[1024,2048]{1,0:T(8,128)(2,1)} fusion(f32[1024,2048]{1,0:T(8,128)} %collective-permute-done.8, f32[1024,2048]{1,0:T(8,128)} %fusion.22, f32[1024,2048]{1,0:T(8,128)S(1)} %fusion.6, f32[1024,2048]{1,0:T(8,128)} %fusion.21), kind=kLoop, calls=%fused_computation.1 | loop fusion | flops 8388608 | bytes 37748736 | tf_op jit(solution)/shard_map/convert_element_type | solution.py:85
  385.5 1.5 collective-permute-start.9
  387.0 1.4 fusion.10
  388.4 5.8 %fusion.18 = f32[1024,2048]{1,0:T(8,128)} fusion(bf16[768,1024]{1,0:T(8,128)(2,1)S(1)} %copy-done.9, bf16[768,2048]{1,0:T(8,128)(2,1)S(1)} %copy-done.2), kind=kOutput, calls=%fused_computation.48 | convolution fusion | flops 3221225472 | bytes 13107200 | tf_op jit(solution)/shard_map/dot_general | solution.py:24
  394.2 7.3 %fusion.19 = f32[1024,2048]{1,0:T(8,128)} fusion(bf16[576,1024]{1,0:T(8,128)(2,1)S(1)} %multiply_convert_fusion.1, bf16[576,2048]{1,0:T(8,128)(2,1)} %collective-permute-done.3), kind=kOutput, calls=%fused_computation.49 | convolution fusion | flops 2415919104 | bytes 11927552 | tf_op jit(solution)/shard_map/dot_general | solution.py:24
  401.5 13.6 %add_add_fusion.2 = f32[1024,2048]{1,0:T(8,128)} fusion(f32[1024,2048]{1,0:T(8,128)} %collective-permute-done.7, f32[1024,2048]{1,0:T(8,128)} %fusion.19, f32[1024,2048]{1,0:T(8,128)S(1)} %fusion.10, f32[1024,2048]{1,0:T(8,128)} %fusion.18), kind=kLoop, calls=%fused_computation.4 | loop fusion | flops 6291456 | bytes 41943040 | tf_op jit(solution)/shard_map/add | solution.py:87
  415.1 62.8 %collective-permute-done.9 = bf16[1024,2048]{1,0:T(8,128)(2,1)} collective-permute-done((bf16[1024,2048]{1,0:T(8,128)(2,1)}, bf16[1024,2048]{1,0:T(8,128)(2,1)}, u32[]{:S(2)}, u32[]{:S(2)}) %collective-permute-start.9) | collective-permute-done | bytes 4194336 | tf_op jit(solution)/shard_map/ppermute | solution.py:30
  477.9 10.1 %convert_add_fusion = f32[1024,2048]{1,0:T(8,128)} fusion(f32[1024,2048]{1,0:T(8,128)} %add_add_fusion.2, bf16[1024,2048]{1,0:T(8,128)(2,1)} %collective-permute-done.9), kind=kLoop, calls=%fused_computation | loop fusion | flops 4194304 | bytes 20971520 | tf_op jit(solution)/shard_map/add | solution.py:88
  (36 shorter events, 1.9 us)
Async XLA Ops:
  6.5 78.1 %all-gather.11.cloned.1.call-start = ((), (), s32[]{:S(2)}) async-start(), calls=%async_computation.3 | async-start | bytes 3932160 | tf_op jit(solution)/shard_map/all_gather | solution.py:63
  8.6 139.8 %all-gather.9.cloned.1.call-start = ((), (), s32[]{:S(2)}) async-start(), calls=%async_computation.2 | async-start | bytes 3932160 | tf_op jit(solution)/shard_map/all_gather | solution.py:70
  8.7 71.5 %collective-permute-start = (bf16[192,8192]{1,0:T(8,128)(2,1)}, bf16[192,8192]{1,0:T(8,128)(2,1)S(1)}, u32[]{:S(2)}, u32[]{:S(2)}) collective-permute-start(bf16[192,8192]{1,0:T(8,128)(2,1)} %param.6), channel_id=1, source_target_pairs={{0,1},{1,0},{2,3},{3,2},{4,5},{5,4},{6,7},{7,6},{8,9},{9,8},{10,11... | collective-permute-start | bytes 9437192 | tf_op jit(solution)/shard_map/ppermute | solution.py:30
  30.0 50.2 %collective-permute-start.2 = (f32[576]{0:T(1024)S(1)}, f32[576]{0:T(1024)S(1)}, u32[]{:S(2)}, u32[]{:S(2)}) collective-permute-start(f32[576]{0:T(1024)S(1)} %fusion.16), channel_id=1, source_target_pairs={{0,1},{1,0},{2,3},{3,2},{4,5},{5,4},{6,7},{7,6},{8,9},{9,8},{10,11... | collective-permute-start | bytes 6920 | tf_op jit(solution)/shard_map/ppermute | solution.py:30
  30.4 49.8 %collective-permute-start.1 = (f32[192]{0:T(256)S(1)}, f32[192]{0:T(256)S(1)}, u32[]{:S(2)}, u32[]{:S(2)}) collective-permute-start(f32[192]{0:T(256)S(1)} %get-tuple-element.14), channel_id=1, source_target_pairs={{0,1},{1,0},{2,3},{3,2},{4,5},{5,4},{6,7},{7,6},{8,9},{9,8},{10,11... | collective-permute-start | bytes 2312 | tf_op jit(solution)/shard_map/ppermute | solution.py:30
  83.3 128.9 %all-gather.7.cloned.1.call-start = ((), (), s32[]{:S(2)}) async-start(), calls=%async_computation.1 | async-start | bytes 3932160 | tf_op jit(solution)/shard_map/all_gather | solution.py:70
  84.1 191.8 %all-gather.5.cloned.1.call-start = ((), (), s32[]{:S(2)}) async-start(), calls=%async_computation | async-start | bytes 3932160 | tf_op jit(solution)/shard_map/all_gather | solution.py:70
  89.7 202.7 %collective-permute-start.6 = (bf16[576,2048]{1,0:T(8,128)(2,1)}, bf16[576,2048]{1,0:T(8,128)(2,1)}, u32[]{:S(2)}, u32[]{:S(2)}) collective-permute-start(bf16[576,2048]{1,0:T(8,128)(2,1)} %fusion), channel_id=1, source_target_pairs={{0,1},{1,0},{2,3},{3,2},{4,5},{5,4},{6,7},{7,6},{8,9},{9,8},{10,11... | collective-permute-start | bytes 7077896 | tf_op jit(solution)/shard_map/ppermute | solution.py:30
  153.5 138.9 %collective-permute-start.5 = (bf16[576,2048]{1,0:T(8,128)(2,1)}, bf16[576,2048]{1,0:T(8,128)(2,1)}, u32[]{:S(2)}, u32[]{:S(2)}) collective-permute-start(bf16[576,2048]{1,0:T(8,128)(2,1)} %fusion.1), channel_id=1, source_target_pairs={{0,1},{1,0},{2,3},{3,2},{4,5},{5,4},{6,7},{7,6},{8,9},{9,8},{10,11... | collective-permute-start | bytes 7077896 | tf_op jit(solution)/shard_map/ppermute | solution.py:30
  217.2 75.1 %collective-permute-start.4 = (bf16[576,2048]{1,0:T(8,128)(2,1)}, bf16[576,2048]{1,0:T(8,128)(2,1)}, u32[]{:S(2)}, u32[]{:S(2)}) collective-permute-start(bf16[576,2048]{1,0:T(8,128)(2,1)} %fusion.2), channel_id=1, source_target_pairs={{0,1},{1,0},{2,3},{3,2},{4,5},{5,4},{6,7},{7,6},{8,9},{9,8},{10,11... | collective-permute-start | bytes 7077896 | tf_op jit(solution)/shard_map/ppermute | solution.py:30
  280.9 53.3 %collective-permute-start.3 = (bf16[576,2048]{1,0:T(8,128)(2,1)}, bf16[576,2048]{1,0:T(8,128)(2,1)}, u32[]{:S(2)}, u32[]{:S(2)}) collective-permute-start(bf16[576,2048]{1,0:T(8,128)(2,1)} %fusion.3), channel_id=1, source_target_pairs={{0,1},{1,0},{2,3},{3,2},{4,5},{5,4},{6,7},{7,6},{8,9},{9,8},{10,11... | collective-permute-start | bytes 7077896 | tf_op jit(solution)/shard_map/ppermute | solution.py:30
  282.4 1.9 copy-start
  282.4 2.8 copy-start.1
  282.4 3.8 copy-start.3
  288.5 3.9 copy-start.6
  344.6 1.9 copy-start.5
  344.6 2.4 copy-start.7
  344.6 29.1 %collective-permute-start.8 = (f32[1024,2048]{1,0:T(8,128)}, f32[1024,2048]{1,0:T(8,128)}, u32[]{:S(2)}, u32[]{:S(2)}) collective-permute-start(f32[1024,2048]{1,0:T(8,128)} %add_add_fusion), channel_id=1, source_target_pairs={{0,8},{8,0},{1,9},{9,1},{2,10},{10,2},{3,11},{11,3},{4,12},{12,4},... | collective-permute-start | bytes 25165832 | tf_op jit(solution)/shard_map/ppermute | solution.py:30
  358.0 1.9 copy-start.4
  358.0 2.4 copy-start.8
  358.0 43.5 %collective-permute-start.7 = (f32[1024,2048]{1,0:T(8,128)}, f32[1024,2048]{1,0:T(8,128)}, u32[]{:S(2)}, u32[]{:S(2)}) collective-permute-start(f32[1024,2048]{1,0:T(8,128)} %add_add_fusion.1), channel_id=1, source_target_pairs={{0,8},{8,0},{1,9},{9,1},{2,10},{10,2},{3,11},{11,3},{4,12},{12,4},... | collective-permute-start | bytes 25165832 | tf_op jit(solution)/shard_map/ppermute | solution.py:30
  385.5 2.8 copy-start.2
  385.5 2.8 copy-start.9
  385.5 92.4 %collective-permute-start.9 = (bf16[1024,2048]{1,0:T(8,128)(2,1)}, bf16[1024,2048]{1,0:T(8,128)(2,1)}, u32[]{:S(2)}, u32[]{:S(2)}) collective-permute-start(bf16[1024,2048]{1,0:T(8,128)(2,1)} %add_convert_fusion), channel_id=1, source_target_pairs={{0,16},{16,0},{1,17},{17,1},{2,18},{18,2},{3,19},{19,3},{4,20},{20... | collective-permute-start | bytes 12582920 | tf_op jit(solution)/shard_map/ppermute | solution.py:30
Sparse Core Ops, SparseCore 0:
  8.9 66.3 all-gather.10
  83.4 64.9 all-gather.8
  150.0 62.1 all-gather.6
  213.6 62.1 all-gather.4

commit v5 on v4

--- a/solution.py
+++ b/solution.py
@@ -43,7 +43,7 @@
         x = lax.axis_index("rx")
         c = lax.axis_index("rc")
         a = z * n_ay + lax.axis_index("ay")
-        order = [(1 - x) * 2 + (1 - c), x * 2 + (1 - c), (1 - x) * 2 + c, x * 2 + c]
+        order = [(1 - x) * 2 + (1 - c), (1 - x) * 2 + c, x * 2 + (1 - c), x * 2 + c]
         home = (a * width) // rw
         off = (a * width) % rw
 
@@ -72,20 +72,26 @@
             )
             mine.append(piece)
             theirs.append(swap(others(piece), "ay"))
+        own_cols = [lax.dynamic_slice_in_dim(theirs_own, m * rw, rw, axis=1) for m in order]
+        fwd = {}
+        for k in (0, 2):
+            fwd[k + 1] = [swap(own_cols[k], "rc"), swap(mine[k], "rc"), swap(theirs[k], "rc")]
+        s_a = scale(w_a, lax.dynamic_slice_in_dim(theirs_own, a * width, width, axis=1))
         s_mine = scale(w_z, pick(mine))
-        s_a = scale(w_a, lax.dynamic_slice_in_dim(theirs_own, a * width, width, axis=1))
-        early = []
-        for k, m in enumerate(order):
-            cols_a = lax.dynamic_slice_in_dim(theirs_own, m * rw, rw, axis=1)
-            early.append(contract(s_a, cols_a) + contract(s_mine, mine[k]))
         s_b = scale(w_b, pick(theirs))
-        blocks = [early[k] + contract(s_b, theirs[k]) for k in range(len(order))]
-        got_other = swap(blocks[0], "rc")
-        other_x = blocks[2] + got_other
-        got_x = swap(other_x.astype(jnp.bfloat16), "rx")
-        got_own = swap(blocks[1], "rc")
-        own_x = lax.optimization_barrier(blocks[3] + got_own)
-        return own_x + got_x.astype(jnp.float32)
+        p_a = swap(s_a, "rc")
+        p_mine = swap(s_mine, "rc")
+        p_b = swap(s_b, "rc")
+        kept = []
+        for k in (1, 3):
+            f_a, f_mine, f_b = fwd[k]
+            early = (
+                contract(s_a, own_cols[k]) + contract(s_mine, mine[k])
+                + contract(p_a, f_a) + contract(p_mine, f_mine)
+            )
+            kept.append(early + contract(s_b, theirs[k]) + contract(p_b, f_b))
+        got_x = swap(kept[0].astype(jnp.bfloat16), "rx")
+        return kept[1] + got_x.astype(jnp.float32)
 
     return body
 

time: 505 us -> 559 us (1.11)
  matrix products: 54.2 us -> 94.7 us
  waiting for transfers between devices: 325 us -> 349 us
  other arithmetic: 62.9 us -> 53.1 us
    dot_general x12, matrix products: 54.2 us -> 94.7 us  [contract(): lax.dot_general(left, right, (((0,), (0,)), ((), ())), preferred_element_...]
    ppermute x10 -> x17, waiting for transfers between devices: 153 us -> 180 us  [swap(): return lax.ppermute(x, axis, [(0, 1), (1, 0)])]
    convert_element_type x1 -> x0, other arithmetic: 11.8 us -> none  [body(): got_x = swap(other_x.astype(jnp.bfloat16), 'rx')]
    ppermute x10 -> x17, starting transfers between devices: 12.7 us -> 13.1 us  [swap(): return lax.ppermute(x, axis, [(0, 1), (1, 0)])]
    add x2 -> x1, other arithmetic: 23.7 us -> 23.7 us  [body(): return kept[1] + got_x.astype(jnp.float32)]
  transfers between devices with their start and end apart: 14 -> 21, of which waited for: 6 -> 7; matrix products, arithmetic and copies ran while one was open for 21% -> 24% of each run, Pallas kernels for 0% -> 0%
where the time goes in v5:
time: 559 us; the launch traced here: 549 us
  waiting for transfers between devices  349 us (62%)
  matrix products  94.7 us (17%)
  other arithmetic  53.1 us (9%)
  between operations  15.4 us (3%)
  starting transfers between devices  13.2 us (2%)
  blocking collectives  12.3 us (2%)
  local copies, waits for them, and re-layouts  11.3 us (2%)
    ppermute x17, waiting for transfers between devices, swap(): return lax.ppermute(x, axis, [(0, 1), (1, 0)])  180 us
    all_gather x3, waiting for transfers between devices, body(): lax.all_gather(lax.dynamic_slice_in_dim(rest, m * rw, rw, axis=1), 'az',...  168 us
    dot_general x12, matrix products, contract(): lax.dot_general(left, right, (((0,), (0,)), ((), ())), preferred_element_...  94.7 us
    add x1, other arithmetic, body(): return kept[1] + got_x.astype(jnp.float32)  23.7 us
    concatenate x5, other arithmetic, others(): doubled = jnp.concatenate([v, v], axis=0)  20.2 us
    ppermute x17, starting transfers between devices, swap(): return lax.ppermute(x, axis, [(0, 1), (1, 0)])  13.1 us
    unnamed x1, blocking collectives  12.3 us
  transfers between devices with their start and end apart: 21, of which 7 were waited for; matrix products, arithmetic and copies ran while one was open for 24% of the time, Pallas kernels for 0%

profile of v5, /device:TPU:0, one launch (start us, length us, event | category | flops | bytes accessed | tf_op | source)
XLA Modules:
  0.0 549.2 jit_solution(8885403882292197521)
XLA Ops:
  6.5 2.1 constant_dynamic-slice_fusion.1
  8.7 3.0 collective-permute-start
  13.0 0.8 dynamic_slice.69
  13.8 1.3 dynamic-slice
  15.8 0.7 and_select_fusion
  16.6 1.0 select_reduce_fusion
  17.5 0.1 fusion.11
  17.6 12.3 %all-reduce = f32[768]{0:T(1024)S(1)} all-reduce(f32[768]{0:T(1024)S(1)} %get-tuple-element.13), channel_id=1, replica_groups=mesh['rx'=2,'rc'=2,'az'=4,'ay'=2] {'az'}, use_global_device_ids=true, to_apply=%add | all-reduce | flops 768 | bytes 6144
  30.0 0.5 collective-permute-start.2
  30.5 1.6 collective-permute-start.1
  32.1 48.1 %collective-permute-done.1 = f32[192]{0:T(256)S(1)} collective-permute-done((f32[192]{0:T(256)S(1)}, f32[192]{0:T(256)S(1)}, u32[]{:S(2)}, u32[]{:S(2)}) %collective-permute-start.1) | collective-permute-done | bytes 800 | tf_op jit(solution)/shard_map/ppermute | solution.py:30
  80.2 4.2 constant_dynamic-slice_fusion.5
  84.5 0.7 all-gather.7.cloned.1.call-update
  85.3 0.5 all-gather.9.cloned.1.call-update
  85.8 5.0 fusion
  90.8 1.7 collective-permute-start.10
  92.6 57.0 %all-gather.5.cloned.1.call-done = bf16[768,2048]{1,0:T(8,128)(2,1)} async-done(((bf16[192,2048]{1,0:T(8,128)(2,1)}), bf16[768,2048]{1,0:T(8,128)(2,1)}) %all-gather.5.cloned.1.call-update) | async-done | bytes 3145744 | tf_op jit(solution)/shard_map/all_gather | solution.py:70
  149.6 5.0 fusion.3
  154.6 1.5 collective-permute-start.7
  156.1 2.8 constant_dynamic-slice_fusion
  158.9 1.2 multiply_convert_fusion.2
  160.1 0.6 collective-permute-start.3
  160.8 52.6 %all-gather.7.cloned.1.call-done = bf16[768,2048]{1,0:T(8,128)(2,1)} async-done(((bf16[192,2048]{1,0:T(8,128)(2,1)}), bf16[768,2048]{1,0:T(8,128)(2,1)}) %all-gather.7.cloned.1.call-update) | async-done | bytes 3145744 | tf_op jit(solution)/shard_map/all_gather | solution.py:70
  213.4 5.1 fusion.2
  218.4 58.6 %all-gather.9.cloned.1.call-done = bf16[768,2048]{1,0:T(8,128)(2,1)} async-done(((bf16[192,2048]{1,0:T(8,128)(2,1)}), bf16[768,2048]{1,0:T(8,128)(2,1)}) %all-gather.9.cloned.1.call-update) | async-done | bytes 3145744 | tf_op jit(solution)/shard_map/all_gather | solution.py:70
  277.0 5.0 fusion.1
  282.0 1.5 collective-permute-start.8
  283.4 0.6 collective-permute-start.9
  284.0 3.2 multiply_convert_fusion
  287.3 6.2 %fusion.4 = f32[1024,2048]{1,0:T(8,128)} fusion(bf16[192,1024]{1,0:T(8,128)(2,1)S(1)} %multiply_convert_fusion.2, bf16[192,8192]{1,0:T(8,128)(2,1)} %copy-done.3, s32[]{:T(128)S(6)} %select_n.124), kind=kOutput, calls=%fused_computation.18 | convolution fusion | flops 805306368 | bytes 9568260 | tf_op jit(solution)/shard_map/dot_general | solution.py:24
  293.5 6.4 %fusion.18 = f32[1024,2048]{1,0:T(8,128)} fusion(bf16[192,1024]{1,0:T(8,128)(2,1)} %collective-permute-done.3, bf16[192,2048]{1,0:T(8,128)(2,1)} %collective-permute-done.13), kind=kOutput, calls=%fused_computation.47 | convolution fusion | flops 805306368 | bytes 9568256 | tf_op jit(solution)/shard_map/dot_general | solution.py:24
  299.9 5.8 %fusion.17 = f32[1024,2048]{1,0:T(8,128)} fusion(bf16[768,1024]{1,0:T(8,128)(2,1)S(1)} %multiply_convert_fusion, bf16[768,2048]{1,0:T(8,128)(2,1)S(1)} %copy-done.2), kind=kOutput, calls=%fused_computation.46 | convolution fusion | flops 3221225472 | bytes 13107200 | tf_op jit(solution)/shard_map/dot_general | solution.py:24
  305.7 30.8 %collective-permute-done.8 = bf16[576,2048]{1,0:T(8,128)(2,1)} collective-permute-done((bf16[576,2048]{1,0:T(8,128)(2,1)}, bf16[576,2048]{1,0:T(8,128)(2,1)}, u32[]{:S(2)}, u32[]{:S(2)}) %collective-permute-start.8) | collective-permute-done | bytes 2359328 | tf_op jit(solution)/shard_map/ppermute | solution.py:30
  336.4 49.4 %collective-permute-done.9 = bf16[576,2048]{1,0:T(8,128)(2,1)} collective-permute-done((bf16[576,2048]{1,0:T(8,128)(2,1)}, bf16[576,2048]{1,0:T(8,128)(2,1)}, u32[]{:S(2)}, u32[]{:S(2)}) %collective-permute-start.9) | collective-permute-done | bytes 2359328 | tf_op jit(solution)/shard_map/ppermute | solution.py:30
  385.8 3.0 multiply_convert_fusion.1
  388.9 8.5 %fusion.19 = f32[1024,2048]{1,0:T(8,128)} fusion(bf16[768,1024]{1,0:T(8,128)(2,1)S(1)} %collective-permute-done.5, bf16[768,2048]{1,0:T(8,128)(2,1)} %collective-permute-done.14), kind=kOutput, calls=%fused_computation.48 | convolution fusion | flops 3221225472 | bytes 13107200 | tf_op jit(solution)/shard_map/dot_general | solution.py:24
  397.4 7.4 %fusion.20 = f32[1024,2048]{1,0:T(8,128)} fusion(bf16[576,1024]{1,0:T(8,128)(2,1)S(1)} %multiply_convert_fusion.1, bf16[576,2048]{1,0:T(8,128)(2,1)} %collective-permute-done.9), kind=kOutput, calls=%fused_computation.49 | convolution fusion | flops 2415919104 | bytes 11927552 | tf_op jit(solution)/shard_map/dot_general | solution.py:24
  404.8 21.0 %add_convert_fusion = bf16[1024,2048]{1,0:T(8,128)(2,1)} fusion(f32[1024,2048]{1,0:T(8,128)} %fusion.20, f32[1024,2048]{1,0:T(8,128)} %fusion.19, f32[1024,2048]{1,0:T(8,128)} %fusion.18, f32[1024,2048]{1,0:T(8,128)} %fusion.4, f32[1024,2048]{1,0:T(8,128)} %fusion.17, bf16[576,1024]{1,0:T(8,128)(2,1)} %collective-permute-done.11, ...), kind=kOutput, calls=%fused_computation.1 | convolution fusion | flops 2428502016 | bytes 49676288 | tf_op jit(solution)/shard_map/dot_general | solution.py:24
  425.8 1.5 collective-permute-start.16
  427.3 5.7 %fusion.6 = f32[1024,2048]{1,0:T(8,128)} fusion(bf16[192,1024]{1,0:T(8,128)(2,1)S(1)} %multiply_convert_fusion.2, bf16[192,8192]{1,0:T(8,128)(2,1)} %copy-done.3, s32[]{:T(128)S(6)} %select_n.116), kind=kOutput, calls=%fused_computation.20 | convolution fusion | flops 805306368 | bytes 9568260 | tf_op jit(solution)/shard_map/dot_general | solution.py:24
  433.0 0.5 collective-permute-start.12
  433.5 5.8 %fusion.13 = f32[1024,2048]{1,0:T(8,128)} fusion(bf16[192,1024]{1,0:T(8,128)(2,1)} %collective-permute-done.3, bf16[192,2048]{1,0:T(8,128)(2,1)S(1)} %collective-permute-done.4), kind=kOutput, calls=%fused_computation.42 | convolution fusion | flops 805306368 | bytes 9568256 | tf_op jit(solution)/shard_map/dot_general | solution.py:24
  439.3 5.7 %fusion.12 = f32[1024,2048]{1,0:T(8,128)} fusion(bf16[768,1024]{1,0:T(8,128)(2,1)S(1)} %copy-done.5, bf16[768,2048]{1,0:T(8,128)(2,1)S(1)} %copy-done.1), kind=kOutput, calls=%fused_computation.41 | convolution fusion | flops 3221225472 | bytes 13107200 | tf_op jit(solution)/shard_map/dot_general | solution.py:24
  445.0 7.5 %fusion.15 = f32[1024,2048]{1,0:T(8,128)} fusion(bf16[576,1024]{1,0:T(8,128)(2,1)S(1)} %copy-done.7, bf16[576,2048]{1,0:T(8,128)(2,1)} %collective-permute-done.7), kind=kOutput, calls=%fused_computation.44 | convolution fusion | flops 2415919104 | bytes 11927552 | tf_op jit(solution)/shard_map/dot_general | solution.py:24
  452.5 7.7 %fusion.14 = f32[1024,2048]{1,0:T(8,128)} fusion(bf16[768,1024]{1,0:T(8,128)(2,1)S(1)} %copy-done.10, bf16[768,2048]{1,0:T(8,128)(2,1)} %collective-permute-done.6), kind=kOutput, calls=%fused_computation.43 | convolution fusion | flops 3221225472 | bytes 13107200 | tf_op jit(solution)/shard_map/dot_general | solution.py:24
  460.2 7.1 %fusion.16 = f32[1024,2048]{1,0:T(8,128)} fusion(bf16[576,1024]{1,0:T(8,128)(2,1)} %collective-permute-done.11, bf16[576,2048]{1,0:T(8,128)(2,1)S(1)} %collective-permute-done.12), kind=kOutput, calls=%fused_computation.45 | convolution fusion | flops 2415919104 | bytes 11927552 | tf_op jit(solution)/shard_map/dot_general | solution.py:24
  467.3 51.4 %collective-permute-done.16 = bf16[1024,2048]{1,0:T(8,128)(2,1)} collective-permute-done((bf16[1024,2048]{1,0:T(8,128)(2,1)}, bf16[1024,2048]{1,0:T(8,128)(2,1)}, u32[]{:S(2)}, u32[]{:S(2)}) %collective-permute-start.16) | collective-permute-done | bytes 4194336 | tf_op jit(solution)/shard_map/ppermute | solution.py:30
  518.8 23.7 %convert_add_fusion = f32[1024,2048]{1,0:T(8,128)} fusion(bf16[1024,2048]{1,0:T(8,128)(2,1)} %collective-permute-done.16, f32[1024,2048]{1,0:T(8,128)} %fusion.16, f32[1024,2048]{1,0:T(8,128)} %fusion.15, f32[1024,2048]{1,0:T(8,128)} %fusion.14, f32[1024,2048]{1,0:T(8,128)} %fusion.13, f32[1024,2048]{1,0:T(8,128)} %fusion.6, f32[1024,2048]{1,0:T(8,128)} %fusion.12), kind=kLoop, calls=%fused_computation | loop fusion | flops 14680064 | bytes 62914560 | tf_op jit(solution)/shard_map/add | solution.py:94
  (52 shorter events, 0.7 us)
Async XLA Ops:
  6.5 79.3 %all-gather.11.cloned.1.call-start = ((), (), s32[]{:S(2)}) async-start(), calls=%async_computation.3 | async-start | bytes 3932160 | tf_op jit(solution)/shard_map/all_gather | solution.py:63
  8.6 140.9 %all-gather.5.cloned.1.call-start = ((), (), s32[]{:S(2)}) async-start(), calls=%async_computation | async-start | bytes 3932160 | tf_op jit(solution)/shard_map/all_gather | solution.py:70
  8.7 71.5 %collective-permute-start = (bf16[192,8192]{1,0:T(8,128)(2,1)}, bf16[192,8192]{1,0:T(8,128)(2,1)S(1)}, u32[]{:S(2)}, u32[]{:S(2)}) collective-permute-start(bf16[192,8192]{1,0:T(8,128)(2,1)} %param.6), channel_id=1, source_target_pairs={{0,1},{1,0},{2,3},{3,2},{4,5},{5,4},{6,7},{7,6},{8,9},{9,8},{10,11... | collective-permute-start | bytes 9437192 | tf_op jit(solution)/shard_map/ppermute | solution.py:30
  30.0 50.2 %collective-permute-start.2 = (f32[576]{0:T(1024)S(1)}, f32[576]{0:T(1024)S(1)}, u32[]{:S(2)}, u32[]{:S(2)}) collective-permute-start(f32[576]{0:T(1024)S(1)} %fusion.10), channel_id=1, source_target_pairs={{0,1},{1,0},{2,3},{3,2},{4,5},{5,4},{6,7},{7,6},{8,9},{9,8},{10,11... | collective-permute-start | bytes 6920 | tf_op jit(solution)/shard_map/ppermute | solution.py:30
  30.5 49.7 %collective-permute-start.1 = (f32[192]{0:T(256)S(1)}, f32[192]{0:T(256)S(1)}, u32[]{:S(2)}, u32[]{:S(2)}) collective-permute-start(f32[192]{0:T(256)S(1)} %get-tuple-element.14), channel_id=1, source_target_pairs={{0,1},{1,0},{2,3},{3,2},{4,5},{5,4},{6,7},{7,6},{8,9},{9,8},{10,11... | collective-permute-start | bytes 2312 | tf_op jit(solution)/shard_map/ppermute | solution.py:30
  80.2 5.0 copy-start.3
  84.5 128.9 %all-gather.7.cloned.1.call-start = ((), (), s32[]{:S(2)}) async-start(), calls=%async_computation.1 | async-start | bytes 3932160 | tf_op jit(solution)/shard_map/all_gather | solution.py:70
  85.2 191.7 %all-gather.9.cloned.1.call-start = ((), (), s32[]{:S(2)}) async-start(), calls=%async_computation.2 | async-start | bytes 3932160 | tf_op jit(solution)/shard_map/all_gather | solution.py:70
  90.8 196.4 %collective-permute-start.10 = (bf16[576,2048]{1,0:T(8,128)(2,1)}, bf16[576,2048]{1,0:T(8,128)(2,1)}, u32[]{:S(2)}, u32[]{:S(2)}) collective-permute-start(bf16[576,2048]{1,0:T(8,128)(2,1)} %fusion), channel_id=1, source_target_pairs={{0,1},{1,0},{2,3},{3,2},{4,5},{5,4},{6,7},{7,6},{8,9},{9,8},{10,11... | collective-permute-start | bytes 7077896 | tf_op jit(solution)/shard_map/ppermute | solution.py:30
  154.6 6.0 %copy-start = (bf16[768,2048]{1,0:T(8,128)(2,1)S(1)}, bf16[768,2048]{1,0:T(8,128)(2,1)}, u32[]{:S(2)}) copy-start(bf16[768,2048]{1,0:T(8,128)(2,1)} %all-gather.11.cloned.1.call-done) | copy-start | bytes 9437188
  154.6 138.9 %collective-permute-start.7 = (bf16[576,2048]{1,0:T(8,128)(2,1)}, bf16[576,2048]{1,0:T(8,128)(2,1)}, u32[]{:S(2)}, u32[]{:S(2)}) collective-permute-start(bf16[576,2048]{1,0:T(8,128)(2,1)} %fusion.3), channel_id=1, source_target_pairs={{0,1},{1,0},{2,3},{3,2},{4,5},{5,4},{6,7},{7,6},{8,9},{9,8},{10,11... | collective-permute-start | bytes 7077896 | tf_op jit(solution)/shard_map/ppermute | solution.py:30
  158.9 124.5 %collective-permute-start.13 = (bf16[192,2048]{1,0:T(8,128)(2,1)}, bf16[192,2048]{1,0:T(8,128)(2,1)}, u32[]{:S(2)}, u32[]{:S(2)}) collective-permute-start(bf16[192,2048]{1,0:T(8,128)(2,1)} %get-tuple-element.16), channel_id=1, source_target_pairs={{0,8},{8,0},{1,9},{9,1},{2,10},{10,2},{3,11},{11,3},{4,12},{12,4},... | collective-permute-start | bytes 2359304 | tf_op jit(solution)/shard_map/ppermute | solution.py:30
  160.1 121.9 %collective-permute-start.3 = (bf16[192,1024]{1,0:T(8,128)(2,1)S(1)}, bf16[192,1024]{1,0:T(8,128)(2,1)}, u32[]{:S(2)}, u32[]{:S(2)}) collective-permute-start(bf16[192,1024]{1,0:T(8,128)(2,1)S(1)} %multiply_convert_fusion.2), channel_id=1, source_target_pairs={{0,8},{8,0},{1,9},{9,1},{2,10},{10,2},{3,11},{11,3},{4,12},{12,4},... | collective-permute-start | bytes 1179656 | tf_op jit(solution)/shard_map/ppermute | solution.py:30
  160.7 228.2 %collective-permute-start.14 = (bf16[768,2048]{1,0:T(8,128)(2,1)S(1)}, bf16[768,2048]{1,0:T(8,128)(2,1)}, u32[]{:S(2)}, u32[]{:S(2)}) collective-permute-start(bf16[768,2048]{1,0:T(8,128)(2,1)S(1)} %copy-done), channel_id=1, source_target_pairs={{0,8},{8,0},{1,9},{9,1},{2,10},{10,2},{3,11},{11,3},{4,12},{12,4},... | collective-permute-start | bytes 9437192 | tf_op jit(solution)/shard_map/ppermute | solution.py:30
  282.0 54.5 %collective-permute-start.8 = (bf16[576,2048]{1,0:T(8,128)(2,1)}, bf16[576,2048]{1,0:T(8,128)(2,1)}, u32[]{:S(2)}, u32[]{:S(2)}) collective-permute-start(bf16[576,2048]{1,0:T(8,128)(2,1)} %fusion.2), channel_id=1, source_target_pairs={{0,1},{1,0},{2,3},{3,2},{4,5},{5,4},{6,7},{7,6},{8,9},{9,8},{10,11... | collective-permute-start | bytes 7077896 | tf_op jit(solution)/shard_map/ppermute | solution.py:30
  283.4 102.3 %collective-permute-start.9 = (bf16[576,2048]{1,0:T(8,128)(2,1)}, bf16[576,2048]{1,0:T(8,128)(2,1)}, u32[]{:S(2)}, u32[]{:S(2)}) collective-permute-start(bf16[576,2048]{1,0:T(8,128)(2,1)} %fusion.1), channel_id=1, source_target_pairs={{0,1},{1,0},{2,3},{3,2},{4,5},{5,4},{6,7},{7,6},{8,9},{9,8},{10,11... | collective-permute-start | bytes 7077896 | tf_op jit(solution)/shard_map/ppermute | solution.py:30
  287.2 12.7 %copy-start.4 = (bf16[768,1024]{1,0:T(8,128)(2,1)}, bf16[768,1024]{1,0:T(8,128)(2,1)S(1)}, u32[]{:S(2)}) copy-start(bf16[768,1024]{1,0:T(8,128)(2,1)S(1)} %multiply_convert_fusion) | copy-start | bytes 4718596
  287.2 101.6 %collective-permute-start.5 = (bf16[768,1024]{1,0:T(8,128)(2,1)S(1)}, bf16[768,1024]{1,0:T(8,128)(2,1)S(1)}, u32[]{:S(2)}, u32[]{:S(2)}) collective-permute-start(bf16[768,1024]{1,0:T(8,128)(2,1)S(1)} %multiply_convert_fusion), channel_id=1, source_target_pairs={{0,8},{8,0},{1,9},{9,1},{2,10},{10,2},{3,11},{11,3},{4,12},{12,4},... | collective-permute-start | bytes 4718600 | tf_op jit(solution)/shard_map/ppermute | solution.py:30
  293.5 6.4 %copy-start.2 = (bf16[768,2048]{1,0:T(8,128)(2,1)S(1)}, bf16[768,2048]{1,0:T(8,128)(2,1)}, u32[]{:S(2)}) copy-start(bf16[768,2048]{1,0:T(8,128)(2,1)} %all-gather.9.cloned.1.call-done) | copy-start | bytes 9437188
  293.5 111.3 %collective-permute-start.15 = (bf16[576,2048]{1,0:T(8,128)(2,1)}, bf16[576,2048]{1,0:T(8,128)(2,1)}, u32[]{:S(2)}, u32[]{:S(2)}) collective-permute-start(bf16[576,2048]{1,0:T(8,128)(2,1)} %collective-permute-done.10), channel_id=1, source_target_pairs={{0,8},{8,0},{1,9},{9,1},{2,10},{10,2},{3,11},{11,3},{4,12},{12,4},... | collective-permute-start | bytes 7077896 | tf_op jit(solution)/shard_map/ppermute | solution.py:30
  336.4 116.1 %collective-permute-start.6 = (bf16[768,2048]{1,0:T(8,128)(2,1)}, bf16[768,2048]{1,0:T(8,128)(2,1)}, u32[]{:S(2)}, u32[]{:S(2)}) collective-permute-start(bf16[768,2048]{1,0:T(8,128)(2,1)} %all-gather.7.cloned.1.call-done), channel_id=1, source_target_pairs={{0,8},{8,0},{1,9},{9,1},{2,10},{10,2},{3,11},{11,3},{4,12},{12,4},... | collective-permute-start | bytes 9437192 | tf_op jit(solution)/shard_map/ppermute | solution.py:30
  388.8 8.6 %copy-start.6 = (bf16[576,1024]{1,0:T(8,128)(2,1)}, bf16[576,1024]{1,0:T(8,128)(2,1)S(1)}, u32[]{:S(2)}) copy-start(bf16[576,1024]{1,0:T(8,128)(2,1)S(1)} %multiply_convert_fusion.1) | copy-start | bytes 3538948
  388.8 16.0 %collective-permute-start.11 = (bf16[576,1024]{1,0:T(8,128)(2,1)S(1)}, bf16[576,1024]{1,0:T(8,128)(2,1)}, u32[]{:S(2)}, u32[]{:S(2)}) collective-permute-start(bf16[576,1024]{1,0:T(8,128)(2,1)S(1)} %multiply_convert_fusion.1), channel_id=1, source_target_pairs={{0,8},{8,0},{1,9},{9,1},{2,10},{10,2},{3,11},{11,3},{4,12},{12,4},... | collective-permute-start | bytes 3538952 | tf_op jit(solution)/shard_map/ppermute | solution.py:30
  388.9 8.5 %copy-start.9 = (bf16[768,1024]{1,0:T(8,128)(2,1)}, bf16[768,1024]{1,0:T(8,128)(2,1)S(1)}, u32[]{:S(2)}) copy-start(bf16[768,1024]{1,0:T(8,128)(2,1)S(1)} %collective-permute-done.5) | copy-start | bytes 4718596
  404.8 22.5 %copy-start.8 = (bf16[192,2048]{1,0:T(8,128)(2,1)S(1)}, bf16[192,2048]{1,0:T(8,128)(2,1)}, u32[]{:S(2)}) copy-start(bf16[192,2048]{1,0:T(8,128)(2,1)} %get-tuple-element.15) | copy-start | bytes 2359300
  425.8 93.0 %collective-permute-start.16 = (bf16[1024,2048]{1,0:T(8,128)(2,1)}, bf16[1024,2048]{1,0:T(8,128)(2,1)}, u32[]{:S(2)}, u32[]{:S(2)}) collective-permute-start(bf16[1024,2048]{1,0:T(8,128)(2,1)} %add_convert_fusion), channel_id=1, source_target_pairs={{0,16},{16,0},{1,17},{17,1},{2,18},{18,2},{3,19},{19,3},{4,20},{20... | collective-permute-start | bytes 12582920 | tf_op jit(solution)/shard_map/ppermute | solution.py:30
  427.3 6.2 %collective-permute-start.4 = (bf16[192,2048]{1,0:T(8,128)(2,1)S(1)}, bf16[192,2048]{1,0:T(8,128)(2,1)S(1)}, u32[]{:S(2)}, u32[]{:S(2)}) collective-permute-start(bf16[192,2048]{1,0:T(8,128)(2,1)S(1)} %copy-done.8), channel_id=1, source_target_pairs={{0,8},{8,0},{1,9},{9,1},{2,10},{10,2},{3,11},{11,3},{4,12},{12,4},... | collective-permute-start | bytes 2359304 | tf_op jit(solution)/shard_map/ppermute | solution.py:30
  433.0 6.3 %copy-start.1 = (bf16[768,2048]{1,0:T(8,128)(2,1)S(1)}, bf16[768,2048]{1,0:T(8,128)(2,1)}, u32[]{:S(2)}) copy-start(bf16[768,2048]{1,0:T(8,128)(2,1)} %all-gather.5.cloned.1.call-done) | copy-start | bytes 9437188
  433.0 6.3 %copy-start.5 = (bf16[768,1024]{1,0:T(8,128)(2,1)S(1)}, bf16[768,1024]{1,0:T(8,128)(2,1)}, u32[]{:S(2)}) copy-start(bf16[768,1024]{1,0:T(8,128)(2,1)} %copy-done.4) | copy-start | bytes 4718596
  433.0 27.2 %collective-permute-start.12 = (bf16[576,2048]{1,0:T(8,128)(2,1)}, bf16[576,2048]{1,0:T(8,128)(2,1)S(1)}, u32[]{:S(2)}, u32[]{:S(2)}) collective-permute-start(bf16[576,2048]{1,0:T(8,128)(2,1)} %collective-permute-done.8), channel_id=1, source_target_pairs={{0,8},{8,0},{1,9},{9,1},{2,10},{10,2},{3,11},{11,3},{4,12},{12,4},... | collective-permute-start | bytes 7077896 | tf_op jit(solution)/shard_map/ppermute | solution.py:30
  439.3 5.7 %copy-start.7 = (bf16[576,1024]{1,0:T(8,128)(2,1)S(1)}, bf16[576,1024]{1,0:T(8,128)(2,1)}, u32[]{:S(2)}) copy-start(bf16[576,1024]{1,0:T(8,128)(2,1)} %copy-done.6) | copy-start | bytes 3538948
  445.0 7.5 %copy-start.10 = (bf16[768,1024]{1,0:T(8,128)(2,1)S(1)}, bf16[768,1024]{1,0:T(8,128)(2,1)}, u32[]{:S(2)}) copy-start(bf16[768,1024]{1,0:T(8,128)(2,1)} %copy-done.9) | copy-start | bytes 4718596
Sparse Core Ops, SparseCore 0:
  8.9 66.3 all-gather.10
  84.6 64.9 all-gather.4
  151.2 62.1 all-gather.6
  214.8 62.1 all-gather.8
